TPU v7x, 256 devices: a whole 4x4x8 slice. The times are simulated.
256 devices in a mesh: feat: 64 (over x, z, core), rep: 4 (over y).
Axes of the slice: x: 4, y: 4, z: 8, core: 2. Of those that a mesh axis runs over, the one named last changes fastest.
Arguments:
- features: bfloat16 [4, 128, 32768], P('rep', 'feat'), may hold values from -6 to 6
- neighbors_one: int32 [4, 15, 16384], P('rep'), may hold values from 0 to 32767, as said below
- weight_one: bfloat16 [2, 128, 256], P(None, 'feat'), may hold values from -0.375 to 0.375
- weight_two: bfloat16 [2, 256, 256], replicated, may hold values from -0.25 to 0.25
- send_rows: int32 [4, 64, 64, 32], P('rep', 'feat'), may hold values from 0 to 255
- halo_count: int32 [4, 64, 64], P('rep', 'feat'), may hold values from 1 to 32, as said below
- neighbors_two: int32 [4, 10, 16384], P('rep', None, 'feat'), may hold values from 0 to 2303, as said below
- cotangent: bfloat16 [4, 16384, 256], P('rep', 'feat'), may hold values from -6 to 6
Outputs:
- hidden_two: bfloat16 [4, 16384, 256], P('rep', 'feat')
- grad_one: float32 [2, 128, 256], P(None, 'feat')
- grad_two: float32 [2, 256, 256], replicated
Inputs may be any that keep to these rules, and one draw needn't show every extreme that they name: neighbors_one[r, k, v] lies in the block of sources from 2 * 512 * (v // 512) to 2 * 512 * (v // 512) + 2 * 512 - 1. halo_count[r, p, q] is how many halo slots shard p fills for shard q; in every replica one shard q receives exactly 32 from every shard, every other count is at most 24. send_rows[r, p, q, j] is a local row of shard p; entries with j >= halo_count[r, p, q] are ignored. `neighbors_two`: an entry below 256 is a local row; an entry 256 + p * 32 + j is a halo slot with j < halo_count[r, p, q] for the seed's shard q; every such live slot is named at least once on its shard.
All inputs are finite; a program needn't handle non-finite values.
Results may differ from a plain program's by a relative error of at most 0.0051.
Values may be sent and summed in bfloat16 or wider, within the bound.
No kernel may reach another device: no remote copies, remote signals or barrier semaphores. Data moves between devices by JAX's collectives and lax.ppermute only.
A program may use at most 64 MiB of HBM per device.

v0:
```python
import math

import jax
import jax.numpy as jnp
from jax import lax
from jax.sharding import PartitionSpec as P

BLOCK_NODES = 512


def activate(pre):
    return jnp.where(pre > 0.0, pre, jnp.expm1(jnp.minimum(pre, 0.0)))


def elu_slope(pre):
    return jnp.where(pre > 0.0, jnp.ones_like(pre), jnp.exp(jnp.minimum(pre, 0.0)))


def to_nodes(stacked):
    return lax.all_to_all(stacked, "feat", split_axis=2, concat_axis=1, tiled=True)


def block_aggregate(table_x, index_one):
    columns = table_x.shape[0]
    fanout_one = index_one.shape[0]
    layer_rows = index_one.shape[1]
    block_rows = BLOCK_NODES
    span_width = 2 * block_rows
    blocks_total = layer_rows // block_rows
    group_size = math.gcd(blocks_total, 4)
    turn_count = blocks_total // group_size
    table_parts = jnp.transpose(
        table_x.reshape(columns, turn_count, group_size, span_width), (1, 0, 2, 3)
    )
    block_base = (jnp.arange(blocks_total, dtype=jnp.int32) * span_width).reshape(
        turn_count, group_size
    )
    relative = (
        index_one.reshape(fanout_one, turn_count, group_size, block_rows)
        - block_base[None, :, :, None]
    )
    relative = jnp.transpose(relative, (1, 0, 2, 3))

    def one_turn(pair):
        table_part, relative_part = pair
        positions = lax.broadcasted_iota(jnp.int32, (group_size, block_rows, span_width), 2)
        tallies = jnp.zeros((group_size, block_rows, span_width), jnp.bfloat16)
        for sample in range(fanout_one):
            tallies = tallies + (relative_part[sample][:, :, None] == positions).astype(
                jnp.bfloat16
            )
        summed = jnp.einsum("cgs,gvs->cgv", table_part, tallies, preferred_element_type=jnp.float32)
        return (summed / fanout_one).astype(jnp.bfloat16)

    gathered = lax.map(one_turn, (table_parts, relative))
    return jnp.transpose(gathered, (1, 0, 2, 3)).reshape(columns, layer_rows)


def on_device(
    features, neighbors_one, weight_one, weight_two, send_rows, halo_count, neighbors_two, cotangent
):
    feat_devs = lax.axis_size("feat")
    rep_devs = lax.axis_size("rep")
    table_x = features[0]
    index_one = neighbors_one[0]
    layer_rows = index_one.shape[1]
    node_count = layer_rows // feat_devs
    hidden_width = weight_one.shape[2]
    aggregate_one = block_aggregate(table_x, index_one)
    stacked = jnp.stack([table_x[:, :layer_rows], aggregate_one])
    node_feats = None
    node_feats = to_nodes(stacked)
    full_weight = lax.all_gather(weight_one, "feat", axis=1, tiled=True)
    pre_one = jnp.einsum("sfr,sfh->rh", node_feats, full_weight, preferred_element_type=jnp.float32)
    hidden_one = activate(pre_one).astype(jnp.bfloat16)
    send_slots = send_rows[0, 0]
    counts = halo_count[0, 0]
    capacity = send_slots.shape[1]
    live_slots = lax.broadcasted_iota(jnp.int32, send_slots.shape, 1) < counts[:, None]
    outgoing = jnp.where(
        live_slots[:, :, None], hidden_one[send_slots], jnp.zeros((), jnp.bfloat16)
    )
    incoming = lax.all_to_all(outgoing, "feat", split_axis=0, concat_axis=0, tiled=True)
    table_two = jnp.concatenate(
        [hidden_one, incoming.reshape(feat_devs * capacity, hidden_width)], axis=0
    )
    index_two = neighbors_two[0]
    fanout_two = index_two.shape[0]
    seed_rows = index_two.shape[1]
    summed_two = jnp.zeros((seed_rows, hidden_width), jnp.float32)
    for sample in range(fanout_two):
        summed_two = summed_two + table_two[index_two[sample]].astype(jnp.float32)
    aggregate_two = (summed_two / fanout_two).astype(jnp.bfloat16)
    pre_two = jnp.dot(hidden_one, weight_two[0], preferred_element_type=jnp.float32) + jnp.dot(
        aggregate_two, weight_two[1], preferred_element_type=jnp.float32
    )
    hidden_two = activate(pre_two).astype(jnp.bfloat16)
    grad_scale = 1.0 / math.sqrt(rep_devs * feat_devs * seed_rows)
    slope_two = (cotangent[0].astype(jnp.float32) * elu_slope(pre_two) * grad_scale).astype(
        jnp.bfloat16
    )
    local_two = jnp.stack(
        [
            jnp.einsum("rh,rk->hk", hidden_one, slope_two, preferred_element_type=jnp.float32),
            jnp.einsum("rh,rk->hk", aggregate_two, slope_two, preferred_element_type=jnp.float32),
        ]
    )
    grad_two = lax.psum(local_two, ("feat", "rep"))
    back_self = jnp.einsum(
        "rk,hk->rh", slope_two, weight_two[0], preferred_element_type=jnp.float32
    )
    back_agg = (
        jnp.einsum("rk,hk->rh", slope_two, weight_two[1], preferred_element_type=jnp.float32)
        / fanout_two
    )
    grad_table = jnp.zeros((table_two.shape[0], hidden_width), jnp.float32)
    for sample in range(fanout_two):
        grad_table = grad_table.at[index_two[sample]].add(back_agg)
    grad_table = grad_table.at[:seed_rows].add(back_self)
    returned = lax.all_to_all(
        grad_table[node_count:].reshape(feat_devs, capacity, hidden_width).astype(jnp.bfloat16),
        "feat",
        split_axis=0,
        concat_axis=0,
        tiled=True,
    ).astype(jnp.float32)
    returned = jnp.where(live_slots[:, :, None], returned, 0.0)
    back_one = grad_table[:node_count].at[send_slots].add(returned)
    slope_one = (back_one * elu_slope(pre_one)).astype(jnp.bfloat16)
    first_local = jnp.einsum(
        "scr,rh->sch",
        stacked,
        lax.all_gather(slope_one, "feat", axis=0, tiled=True),
        preferred_element_type=jnp.float32,
    )
    grad_one = lax.psum(first_local, "rep")
    return (hidden_two[None], grad_one, grad_two)


def solution(mesh):
    return jax.shard_map(
        on_device,
        mesh=mesh,
        in_specs=(
            P("rep", "feat", None),
            P("rep", None, None),
            P(None, "feat", None),
            P(),
            P("rep", "feat", None, None),
            P("rep", "feat", None),
            P("rep", None, "feat"),
            P("rep", "feat", None),
        ),
        out_specs=(P("rep", "feat", None), P(None, "feat", None), P()),
        check_vma=False,
    )
```

profile of v0, /device:TPU:1, one launch (start us, length us, event | category | flops | bytes accessed | tf_op | source)
XLA Modules:
  0.0 701.3 jit_solution(11061386898485496683)
XLA Ops:
  8.0 3.6 reduce.2
  12.6 151.7 %while.11 = (s32[]{:T(128)}, bf16[8,2,4,512]{3,1,2,0:T(2,128)(2,1)S(1)}, s32[8,15,4,512]{3,2,0,1:T(4,128)S(1)}, bf16[8,2,4,1024]{3,1,2,0:T(2,128)(2,1)S(1)}, s32[]{:T(128)}) while((s32[]{:T(128)}, bf16[8,2,4,512]{3,1,2,0:T(2,128)(2,1)S(1)}, s32[8,15,4,512]{3,2,0,1:T(4,128)S(1)}, bf16[8,2,4,1024]{3,1,2,0:T(2,128)(2,1)S(1)}, s32[]{:T(128)}) %tuple.63), condition=%wide.region_1.2_spmd, body=%wide.region_0.1_spmd.sunk | while | flops 134225920 | bytes 671825 | solution.py:55
  12.7 18.9 %fusion.123 = bf16[8,2,4,512]{3,1,2,0:T(2,128)(2,1)S(1)} fusion(bf16[8,2,4,512]{3,1,2,0:T(2,128)(2,1)S(1)} %get-tuple-element.144, s32[]{:T(128)S(6)} %copy.35, s32[4,512]{1,0:T(4,128)S(1)} %get-tuple-element.123, s32[4,512]{1,0:T(4,128)S(1)} %get-tuple-element.124, s32[4,512]{1,0:T(4,128)S(1)} %get-tuple-element.125, ...), kind=kOutput, calls=%fused_computation.85.clone.3 | convolution fusion | flops 134225920 | bytes 147460 | tf_op jit(solution)/shard_map/while/body/eval_jaxpr/cgs,gvs->cgv/dot_general | solution.py:52
  31.6 18.9 %fusion.123 = bf16[8,2,4,512]{3,1,2,0:T(2,128)(2,1)S(1)} fusion(bf16[8,2,4,512]{3,1,2,0:T(2,128)(2,1)S(1)} %get-tuple-element.144, s32[]{:T(128)S(6)} %copy.35, s32[4,512]{1,0:T(4,128)S(1)} %get-tuple-element.123, s32[4,512]{1,0:T(4,128)S(1)} %get-tuple-element.124, s32[4,512]{1,0:T(4,128)S(1)} %get-tuple-element.125, ...), kind=kOutput, calls=%fused_computation.85.clone.3 | convolution fusion | flops 134225920 | bytes 147460 | tf_op jit(solution)/shard_map/while/body/eval_jaxpr/cgs,gvs->cgv/dot_general | solution.py:52
  50.6 18.9 %fusion.123 = bf16[8,2,4,512]{3,1,2,0:T(2,128)(2,1)S(1)} fusion(bf16[8,2,4,512]{3,1,2,0:T(2,128)(2,1)S(1)} %get-tuple-element.144, s32[]{:T(128)S(6)} %copy.35, s32[4,512]{1,0:T(4,128)S(1)} %get-tuple-element.123, s32[4,512]{1,0:T(4,128)S(1)} %get-tuple-element.124, s32[4,512]{1,0:T(4,128)S(1)} %get-tuple-element.125, ...), kind=kOutput, calls=%fused_computation.85.clone.3 | convolution fusion | flops 134225920 | bytes 147460 | tf_op jit(solution)/shard_map/while/body/eval_jaxpr/cgs,gvs->cgv/dot_general | solution.py:52
  69.5 18.9 %fusion.123 = bf16[8,2,4,512]{3,1,2,0:T(2,128)(2,1)S(1)} fusion(bf16[8,2,4,512]{3,1,2,0:T(2,128)(2,1)S(1)} %get-tuple-element.144, s32[]{:T(128)S(6)} %copy.35, s32[4,512]{1,0:T(4,128)S(1)} %get-tuple-element.123, s32[4,512]{1,0:T(4,128)S(1)} %get-tuple-element.124, s32[4,512]{1,0:T(4,128)S(1)} %get-tuple-element.125, ...), kind=kOutput, calls=%fused_computation.85.clone.3 | convolution fusion | flops 134225920 | bytes 147460 | tf_op jit(solution)/shard_map/while/body/eval_jaxpr/cgs,gvs->cgv/dot_general | solution.py:52
  88.5 18.9 %fusion.123 = bf16[8,2,4,512]{3,1,2,0:T(2,128)(2,1)S(1)} fusion(bf16[8,2,4,512]{3,1,2,0:T(2,128)(2,1)S(1)} %get-tuple-element.144, s32[]{:T(128)S(6)} %copy.35, s32[4,512]{1,0:T(4,128)S(1)} %get-tuple-element.123, s32[4,512]{1,0:T(4,128)S(1)} %get-tuple-element.124, s32[4,512]{1,0:T(4,128)S(1)} %get-tuple-element.125, ...), kind=kOutput, calls=%fused_computation.85.clone.3 | convolution fusion | flops 134225920 | bytes 147460 | tf_op jit(solution)/shard_map/while/body/eval_jaxpr/cgs,gvs->cgv/dot_general | solution.py:52
  107.5 18.9 %fusion.123 = bf16[8,2,4,512]{3,1,2,0:T(2,128)(2,1)S(1)} fusion(bf16[8,2,4,512]{3,1,2,0:T(2,128)(2,1)S(1)} %get-tuple-element.144, s32[]{:T(128)S(6)} %copy.35, s32[4,512]{1,0:T(4,128)S(1)} %get-tuple-element.123, s32[4,512]{1,0:T(4,128)S(1)} %get-tuple-element.124, s32[4,512]{1,0:T(4,128)S(1)} %get-tuple-element.125, ...), kind=kOutput, calls=%fused_computation.85.clone.3 | convolution fusion | flops 134225920 | bytes 147460 | tf_op jit(solution)/shard_map/while/body/eval_jaxpr/cgs,gvs->cgv/dot_general | solution.py:52
  126.4 18.9 %fusion.123 = bf16[8,2,4,512]{3,1,2,0:T(2,128)(2,1)S(1)} fusion(bf16[8,2,4,512]{3,1,2,0:T(2,128)(2,1)S(1)} %get-tuple-element.144, s32[]{:T(128)S(6)} %copy.35, s32[4,512]{1,0:T(4,128)S(1)} %get-tuple-element.123, s32[4,512]{1,0:T(4,128)S(1)} %get-tuple-element.124, s32[4,512]{1,0:T(4,128)S(1)} %get-tuple-element.125, ...), kind=kOutput, calls=%fused_computation.85.clone.3 | convolution fusion | flops 134225920 | bytes 147460 | tf_op jit(solution)/shard_map/while/body/eval_jaxpr/cgs,gvs->cgv/dot_general | solution.py:52
  145.4 18.9 %fusion.123 = bf16[8,2,4,512]{3,1,2,0:T(2,128)(2,1)S(1)} fusion(bf16[8,2,4,512]{3,1,2,0:T(2,128)(2,1)S(1)} %get-tuple-element.144, s32[]{:T(128)S(6)} %copy.35, s32[4,512]{1,0:T(4,128)S(1)} %get-tuple-element.123, s32[4,512]{1,0:T(4,128)S(1)} %get-tuple-element.124, s32[4,512]{1,0:T(4,128)S(1)} %get-tuple-element.125, ...), kind=kOutput, calls=%fused_computation.85.clone.3 | convolution fusion | flops 134225920 | bytes 147460 | tf_op jit(solution)/shard_map/while/body/eval_jaxpr/cgs,gvs->cgv/dot_general | solution.py:52
  164.5 12.9 %copy.17 = bf16[2,2,16384]{1,0,2:T(2,128)(2,1)} copy(bf16[2,2,16384]{2,1,0:T(2,128)(2,1)S(1)} %pad_maximum_fusion.2) | data formatting | bytes 262144 | tf_op jit(solution)/shard_map/stack | solution.py:70
  177.5 13.7 %reshape.627 = bf16[64,2,512]{2,1,0:T(2,128)(2,1)} reshape(bf16[16384,2,2]{2,1,0:T(2,128)(2,1)} %bitcast.148) | data formatting | bytes 262144
  191.2 13.0 %all-to-all-start = ((bf16[64,2,512]{2,1,0:T(2,128)(2,1)}), bf16[64,2,512]{2,1,0:T(2,128)(2,1)S(1)}, u32[]{:S(2)}, u32[]{:S(2)}) async-start(bf16[64,2,512]{2,1,0:T(2,128)(2,1)} %reshape.627), calls=%async_computation | async-start | bytes 262144 | tf_op jit(solution)/shard_map/all_to_all | solution.py:20
  204.4 50.8 %all_gather.6 = bf16[2,128,256]{2,0,1:T(2,128)(2,1)S(1)} all-gather(bf16[2,2,256]{2,0,1:T(2,128)(2,1)S(1)} %copy.19), channel_id=1, replica_groups=mesh['feat'=64,'rep'=4] {'feat'}, dimensions={1}, use_global_device_ids=true | all-gather | bytes 133120 | tf_op jit(solution)/shard_map/all_gather | solution.py:73
  255.2 19.1 %reshape.628 = bf16[16384,2,2]{2,1,0:T(2,128)(2,1)} reshape(bf16[64,2,512]{2,1,0:T(2,128)(2,1)S(1)} %all-to-all-done) | data formatting | bytes 262144
  274.3 16.5 %copy.18 = bf16[2,2,64,256]{3,0,1,2:T(2,128)(2,1)S(1)} copy(bf16[2,2,64,256]{1,0,3,2:T(2,128)(2,1)} %bitcast.149) | data formatting | bytes 262144 | tf_op jit(solution)/shard_map/all_to_all | solution.py:20
  291.8 7.5 %gather_fusion = bf16[2048,256]{1,0:T(8,128)(2,1)S(1)} fusion(bf16[256,256]{1,0:T(8,128)(2,1)S(1)} %get-tuple-element.81, s32[2048]{0:T(1024)S(1)} %broadcast_clamp_fusion), kind=kCustom, calls=%fused_computation | custom fusion | bytes 2105344 | tf_op jit(solution)/shard_map/gather | solution.py:81
  299.3 1.3 broadcast_select_fusion
  300.5 7.9 %all-to-all-start.1 = ((bf16[64,32,256]{2,1,0:T(8,128)(2,1)}), bf16[64,32,256]{2,1,0:T(8,128)(2,1)S(1)}, u32[]{:S(2)}, u32[]{:S(2)}) async-start(bf16[64,32,256]{2,1,0:T(8,128)(2,1)} %broadcast_select_fusion), calls=%async_computation.1 | async-start | bytes 2097152 | tf_op jit(solution)/shard_map/all_to_all | solution.py:83
  308.8 28.0 %all-to-all-done.1 = bf16[64,32,256]{2,1,0:T(8,128)(2,1)S(1)} async-done(((bf16[64,32,256]{2,1,0:T(8,128)(2,1)}), bf16[64,32,256]{2,1,0:T(8,128)(2,1)S(1)}, u32[]{:S(2)}, u32[]{:S(2)}) %all-to-all-start.1) | async-done | bytes 1048608 | tf_op jit(solution)/shard_map/all_to_all | solution.py:83
  336.9 1.2 gather_fusion.10
  338.1 1.2 gather_fusion.9
  339.2 1.2 gather_fusion.8
  340.4 1.2 gather_fusion.7
  341.5 1.2 gather_fusion.6
  342.7 1.2 gather_fusion.5
  343.8 1.2 gather_fusion.4
  346.1 1.2 gather_fusion.2
  348.6 1.9 fusion.85
  350.7 2.5 scatter_custom_fusion
  353.2 2.8 scatter_fusion
  356.1 2.8 scatter_fusion.1
  358.9 3.0 scatter_fusion.2
  361.9 2.8 scatter_fusion.3
  364.7 2.8 scatter_fusion.4
  367.6 2.8 scatter_fusion.5
  370.4 2.8 scatter_fusion.6
  373.2 2.8 scatter_fusion.7
  376.1 2.8 scatter_fusion.8
  380.0 6.4 all-to-all-start.2
  386.7 28.2 %all-to-all-done.2 = bf16[64,32,256]{2,1,0:T(8,128)(2,1)} async-done(((bf16[64,32,256]{2,1,0:T(8,128)(2,1)}), bf16[64,32,256]{2,1,0:T(8,128)(2,1)}, u32[]{:S(2)}, u32[]{:S(2)}) %all-to-all-start.2) | async-done | bytes 1048608 | tf_op jit(solution)/shard_map/all_to_all | solution.py:120
  414.9 1.6 convert_select_fusion
  416.4 11.9 %scatter_fusion.9 = f32[256,256]{1,0:T(8,128)S(1)} fusion(f32[256,256]{1,0:T(8,128)S(1)} %convolution_add_fusion, s32[2048]{0:T(1024)S(1)} %reshape.446, f32[2048,256]{1,0:T(8,128)S(1)} %bitcast.150), kind=kCustom, calls=%fused_computation.21 | custom fusion | flops 524288 | bytes 6299648 | tf_op jit(solution)/shard_map/scatter-add | solution.py:128
  430.4 79.3 %all-gather.2.cloned.1.call-done = bf16[16384,256]{1,0:T(8,128)(2,1)} async-done(((bf16[256,256]{1,0:T(8,128)(2,1)}), bf16[16384,256]{1,0:T(8,128)(2,1)}) %all-gather.2.cloned.1.call-update) | async-done | bytes 8388624 | tf_op jit(solution)/shard_map/all_gather | solution.py:133
  509.7 4.8 fusion.75
  514.5 9.7 %psum.14 = f32[2,2,256]{2,1,0:T(2,128)} all-reduce(f32[2,2,256]{2,1,0:T(2,128)S(1)} %fusion.75), channel_id=1, replica_groups=mesh['feat'=64,'rep'=4] {'rep'}, use_global_device_ids=true, to_apply=%region_13.14 | all-reduce | flops 1024 | bytes 8192 | tf_op jit(solution)/shard_map/psum | solution.py:136
  524.2 167.6 %all-reduce.2.cloned.1.call-done = f32[2,256,256]{2,1,0:T(8,128)} async-done(((f32[2,256,256]{2,1,0:T(8,128)}), f32[2,256,256]{2,1,0:T(8,128)}) %all-reduce.2.cloned.1.call-update) | async-done | bytes 524304 | tf_op jit(solution)/shard_map/psum | solution.py:108
  691.8 1.9 copy.52
  (79 shorter events, 9.3 us)
Async XLA Ops:
  8.0 4.6 copy-start.2
  177.4 26.7 %copy-start.3 = (s32[1,1,64,32]{2,3,1,0:T(8,128)S(1)}, s32[1,1,64,32]{2,3,1,0:T(8,128)}, u32[]{:S(2)}) copy-start(s32[1,1,64,32]{2,3,1,0:T(8,128)} %param.16) | copy-start | bytes 24580
  177.4 26.7 %copy-start.6 = (s32[1,1,64]{2,1,0:T(1,128)S(1)}, s32[1,1,64]{2,1,0:T(1,128)}, u32[]{:S(2)}) copy-start(s32[1,1,64]{2,1,0:T(1,128)} %param.17) | copy-start | bytes 772
  177.5 26.8 %copy-start.5 = (bf16[2,2,256]{2,1,0:T(2,128)(2,1)S(1)}, bf16[2,2,256]{2,1,0:T(2,128)(2,1)}, u32[]{:S(2)}) copy-start(bf16[2,2,256]{2,1,0:T(2,128)(2,1)} %param.14) | copy-start | bytes 6148
  191.2 64.1 %all-to-all-start = ((bf16[64,2,512]{2,1,0:T(2,128)(2,1)}), bf16[64,2,512]{2,1,0:T(2,128)(2,1)S(1)}, u32[]{:S(2)}, u32[]{:S(2)}) async-start(bf16[64,2,512]{2,1,0:T(2,128)(2,1)} %reshape.627), calls=%async_computation | async-start | bytes 262144 | tf_op jit(solution)/shard_map/all_to_all | solution.py:20
  299.3 9.2 %copy-start.4 = (s32[1,10,256]{2,0,1:T(1,128)S(1)}, s32[1,10,256]{2,0,1:T(1,128)}, u32[]{:S(2)}) copy-start(s32[1,10,256]{2,0,1:T(1,128)} %param.18) | copy-start | bytes 30724
  299.3 9.3 %copy-start = (bf16[2,256,256]{2,1,0:T(8,128)(2,1)S(1)}, bf16[2,256,256]{2,1,0:T(8,128)(2,1)}, u32[]{:S(2)}) copy-start(bf16[2,256,256]{2,1,0:T(8,128)(2,1)} %param.15) | copy-start | bytes 786436
  300.5 36.3 %all-to-all-start.1 = ((bf16[64,32,256]{2,1,0:T(8,128)(2,1)}), bf16[64,32,256]{2,1,0:T(8,128)(2,1)S(1)}, u32[]{:S(2)}, u32[]{:S(2)}) async-start(bf16[64,32,256]{2,1,0:T(8,128)(2,1)} %broadcast_select_fusion), calls=%async_computation.1 | async-start | bytes 2097152 | tf_op jit(solution)/shard_map/all_to_all | solution.py:83
  380.0 34.8 %all-to-all-start.2 = ((bf16[64,32,256]{2,1,0:T(8,128)(2,1)}), bf16[64,32,256]{2,1,0:T(8,128)(2,1)}, u32[]{:S(2)}, u32[]{:S(2)}) async-start(bf16[64,32,256]{2,1,0:T(8,128)(2,1)} %bitcast.57), calls=%async_computation.2 | async-start | bytes 2097152 | tf_op jit(solution)/shard_map/all_to_all | solution.py:120
  386.4 123.3 %all-gather.2.cloned.1.call-start = ((), (), s32[]{:S(2)}) async-start(), calls=%async_computation.3 | async-start | bytes 8519680 | tf_op jit(solution)/shard_map/all_gather | solution.py:133
  416.4 11.9 %copy-start.1 = (f32[256,256]{1,0:T(8,128)S(1)}, f32[256,256]{1,0:T(8,128)}, u32[]{:S(2)}) copy-start(f32[256,256]{1,0:T(8,128)} %get-tuple-element.82) | copy-start | bytes 786436
  429.1 262.7 %all-reduce.2.cloned.1.call-start = ((), (), s32[]{:S(2)}) async-start(), calls=%async_computation.4 | async-start | bytes 1048576 | tf_op jit(solution)/shard_map/psum | solution.py:108
Sparse Core Ops, SparseCore 0:
  429.2 80.4 all-gather.1
Sparse Core Ops, SparseCore 1:
  435.6 256.1 all-reduce.1
where the time goes:
time: 711 us; the launch traced here: 701 us
  waiting for transfers between devices  303 us (43%)
  matrix products  160 us (23%)
  local copies, waits for them, and re-layouts  85.5 us (12%)
  blocking collectives  60.5 us (9%)
  other arithmetic  48.8 us (7%)
  starting transfers between devices  27.3 us (4%)
  between operations  16.1 us (2%)
    psum x1, waiting for transfers between devices, on_device(): grad_two = lax.psum(local_two, ('feat', 'rep'))  168 us
    dot_general x8, matrix products, one_turn(): jnp.einsum('cgs,gvs->cgv', table_part, tallies, preferred_element_type=jn...  151 us
    all_gather x1, waiting for transfers between devices, on_device(): lax.all_gather(slope_one, 'feat', axis=0, tiled=True)  79.3 us
    all_gather x1, blocking collectives, on_device(): full_weight = lax.all_gather(weight_one, 'feat', axis=1, tiled=True)  50.8 us
    unnamed x18, local copies, waits for them, and re-layouts  34.7 us
    all_to_all x1, waiting for transfers between devices, on_device(): lax.all_to_all(grad_table[node_count:].reshape(feat_devs, capacity, hidde...  28.2 us
    scatter-add x10, other arithmetic, on_device(): grad_table = grad_table.at[index_two[sample]].add(back_agg)  28.1 us
    all_to_all x1, waiting for transfers between devices, on_device(): lax.all_to_all(outgoing, 'feat', split_axis=0, concat_axis=0, tiled=True)  28 us
  transfers between devices with their start and end apart: 5, of which 4 were waited for; matrix products, arithmetic and copies ran while one was open for 1% of the time, Pallas kernels for 0%

commit v1 on v0

--- a/solution.py
+++ b/solution.py
@@ -16,63 +16,55 @@
     return jnp.where(pre > 0.0, jnp.ones_like(pre), jnp.exp(jnp.minimum(pre, 0.0)))
 
 
-def to_nodes(stacked):
-    return lax.all_to_all(stacked, "feat", split_axis=2, concat_axis=1, tiled=True)
-
-
-def block_aggregate(table_x, index_one):
-    columns = table_x.shape[0]
-    fanout_one = index_one.shape[0]
-    layer_rows = index_one.shape[1]
-    block_rows = BLOCK_NODES
-    span_width = 2 * block_rows
-    blocks_total = layer_rows // block_rows
-    group_size = math.gcd(blocks_total, 4)
-    turn_count = blocks_total // group_size
-    table_parts = jnp.transpose(
-        table_x.reshape(columns, turn_count, group_size, span_width), (1, 0, 2, 3)
-    )
-    block_base = (jnp.arange(blocks_total, dtype=jnp.int32) * span_width).reshape(
-        turn_count, group_size
-    )
-    relative = (
-        index_one.reshape(fanout_one, turn_count, group_size, block_rows)
-        - block_base[None, :, :, None]
-    )
-    relative = jnp.transpose(relative, (1, 0, 2, 3))
-
-    def one_turn(pair):
-        table_part, relative_part = pair
-        positions = lax.broadcasted_iota(jnp.int32, (group_size, block_rows, span_width), 2)
-        tallies = jnp.zeros((group_size, block_rows, span_width), jnp.bfloat16)
-        for sample in range(fanout_one):
-            tallies = tallies + (relative_part[sample][:, :, None] == positions).astype(
-                jnp.bfloat16
-            )
-        summed = jnp.einsum("cgs,gvs->cgv", table_part, tallies, preferred_element_type=jnp.float32)
-        return (summed / fanout_one).astype(jnp.bfloat16)
-
-    gathered = lax.map(one_turn, (table_parts, relative))
-    return jnp.transpose(gathered, (1, 0, 2, 3)).reshape(columns, layer_rows)
-
-
 def on_device(
     features, neighbors_one, weight_one, weight_two, send_rows, halo_count, neighbors_two, cotangent
 ):
     feat_devs = lax.axis_size("feat")
     rep_devs = lax.axis_size("rep")
+    me = lax.axis_index("feat")
     table_x = features[0]
+    cols_dev, sources = table_x.shape
     index_one = neighbors_one[0]
-    layer_rows = index_one.shape[1]
+    fanout_one, layer_rows = index_one.shape
     node_count = layer_rows // feat_devs
     hidden_width = weight_one.shape[2]
-    aggregate_one = block_aggregate(table_x, index_one)
-    stacked = jnp.stack([table_x[:, :layer_rows], aggregate_one])
-    node_feats = None
-    node_feats = to_nodes(stacked)
-    full_weight = lax.all_gather(weight_one, "feat", axis=1, tiled=True)
-    pre_one = jnp.einsum("sfr,sfh->rh", node_feats, full_weight, preferred_element_type=jnp.float32)
+    span_width = 2 * BLOCK_NODES
+    span_count = sources // span_width
+    nodes_per_span = BLOCK_NODES // node_count
+
+    block_part = jnp.repeat(
+        jnp.transpose(table_x.reshape(cols_dev, span_count, span_width), (1, 0, 2)),
+        nodes_per_span,
+        axis=0,
+    )[: feat_devs]
+    self_part = jnp.transpose(
+        table_x[:, :layer_rows].reshape(cols_dev, feat_devs, node_count), (1, 0, 2)
+    )
+    weight_part = jnp.transpose(weight_one, (1, 0, 2)).reshape(cols_dev, 2 * hidden_width)
+    weight_part = jnp.broadcast_to(weight_part[None], (feat_devs, cols_dev, 2 * hidden_width))
+    outgoing_one = jnp.concatenate([block_part, self_part, weight_part], axis=2)
+    incoming_one = lax.all_to_all(outgoing_one, "feat", split_axis=0, concat_axis=0, tiled=True)
+    gathered = incoming_one.reshape(feat_devs * cols_dev, -1)
+    block_x = gathered[:, :span_width]
+    self_x = gathered[:, span_width : span_width + node_count]
+    full_weight = gathered[:, span_width + node_count :].reshape(-1, 2, hidden_width)
+
+    my_index = lax.dynamic_slice_in_dim(index_one, me * node_count, node_count, axis=1)
+    block_start = (me * node_count) // BLOCK_NODES * span_width
+    relative = my_index - block_start
+    positions = lax.broadcasted_iota(jnp.int32, (node_count, span_width), 1)
+    tallies = jnp.zeros((node_count, span_width), jnp.float32)
+    for sample in range(fanout_one):
+        tallies = tallies + (relative[sample][:, None] == positions).astype(jnp.float32)
+    tallies = tallies.astype(jnp.bfloat16)
+    summed_one = jnp.einsum("fs,vs->fv", block_x, tallies, preferred_element_type=jnp.float32)
+    aggregate_one = (summed_one / fanout_one).astype(jnp.bfloat16)
+
+    pre_one = jnp.einsum(
+        "fv,fh->vh", self_x, full_weight[:, 0], preferred_element_type=jnp.float32
+    ) + jnp.einsum("fv,fh->vh", aggregate_one, full_weight[:, 1], preferred_element_type=jnp.float32)
     hidden_one = activate(pre_one).astype(jnp.bfloat16)
+
     send_slots = send_rows[0, 0]
     counts = halo_count[0, 0]
     capacity = send_slots.shape[1]
@@ -105,7 +97,6 @@
             jnp.einsum("rh,rk->hk", aggregate_two, slope_two, preferred_element_type=jnp.float32),
         ]
     )
-    grad_two = lax.psum(local_two, ("feat", "rep"))
     back_self = jnp.einsum(
         "rk,hk->rh", slope_two, weight_two[0], preferred_element_type=jnp.float32
     )
@@ -127,13 +118,25 @@
     returned = jnp.where(live_slots[:, :, None], returned, 0.0)
     back_one = grad_table[:node_count].at[send_slots].add(returned)
     slope_one = (back_one * elu_slope(pre_one)).astype(jnp.bfloat16)
-    first_local = jnp.einsum(
-        "scr,rh->sch",
-        stacked,
-        lax.all_gather(slope_one, "feat", axis=0, tiled=True),
-        preferred_element_type=jnp.float32,
+    local_one = jnp.stack(
+        [
+            jnp.einsum("fv,vh->fh", self_x, slope_one, preferred_element_type=jnp.float32),
+            jnp.einsum("fv,vh->fh", aggregate_one, slope_one, preferred_element_type=jnp.float32),
+        ]
     )
-    grad_one = lax.psum(first_local, "rep")
+
+    one_part = jnp.transpose(
+        local_one.reshape(2, feat_devs, cols_dev, hidden_width), (1, 0, 2, 3)
+    ).reshape(feat_devs, -1)
+    two_part = local_two.reshape(feat_devs, -1)
+    outgoing_grad = jnp.concatenate([one_part, two_part], axis=1)
+    incoming_grad = lax.all_to_all(outgoing_grad, "feat", split_axis=0, concat_axis=0, tiled=True)
+    reduced = lax.psum(jnp.sum(incoming_grad, axis=0), "rep")
+    one_size = one_part.shape[1]
+    grad_one = reduced[:one_size].reshape(2, cols_dev, hidden_width)
+    grad_two = lax.all_gather(reduced[one_size:], "feat", axis=0, tiled=True).reshape(
+        local_two.shape
+    )
     return (hidden_two[None], grad_one, grad_two)
 
 

time: 711 us -> 278 us (0.39)
  waiting for transfers between devices: 303 us -> 69 us
  matrix products: 160 us -> 7.54 us
  local copies, waits for them, and re-layouts: 85.5 us -> 26.5 us
  blocking collectives: 60.5 us -> 95.4 us
  between operations: 16.1 us -> 1.93 us
    psum x1 -> x0, waiting for transfers between devices: 168 us -> none  [on_device(): grad_two = lax.psum(local_two, ('feat', 'rep'))]
    dot_general x10 -> x5, matrix products: 157 us -> 4.56 us  [the longest x1 2.2 us: on_device(): jnp.einsum('fs,vs->fv', block_x, tallies, preferred_element_type=jnp.floa...]
    all_gather x1 -> x0, waiting for transfers between devices: 79.3 us -> none  [on_device(): lax.all_gather(slope_one, 'feat', axis=0, tiled=True)]
    unnamed x18 -> x57, local copies, waits for them, and re-layouts: 34.7 us -> 1.45 us
    all_to_all x0 -> x1, blocking collectives: none -> 28.9 us  [on_device(): lax.all_to_all(outgoing_grad, 'feat', split_axis=0, concat_axis=0, tiled=...]
    all_to_all x1, local copies, waits for them, and re-layouts: 16.5 us -> 0.54 us  [on_device(): lax.all_to_all(outgoing_grad, 'feat', split_axis=0, concat_axis=0, tiled=...]
    all_to_all x1, waiting for transfers between devices: 0.01 us -> 14.8 us  [on_device(): lax.all_to_all(outgoing_one, 'feat', split_axis=0, concat_axis=0, tiled=T...]
    another operation x3 -> x2, local copies, waits for them, and re-layouts: 13.7 us -> 0.15 us  [on_device(): jnp.stack([jnp.einsum('fv,vh->fh', self_x, slope_one, preferred_element_t...]
  transfers between devices with their start and end apart: 5 -> 3, of which waited for: 4 -> 3; matrix products, arithmetic and copies ran while one was open for 1% -> 1% of each run, Pallas kernels for 0% -> 0%
where the time goes in v1:
time: 278 us; the launch traced here: 273 us
  blocking collectives  95.4 us (34%)
  waiting for transfers between devices  69 us (25%)
  other arithmetic  46.2 us (17%)
  local copies, waits for them, and re-layouts  26.5 us (10%)
  starting transfers between devices  25.9 us (9%)
  matrix products  7.54 us (3%)
    all_gather x1, blocking collectives, on_device(): lax.all_gather(reduced[one_size:], 'feat', axis=0, tiled=True)  53.1 us
    all_to_all x1, blocking collectives, on_device(): lax.all_to_all(outgoing_grad, 'feat', split_axis=0, concat_axis=0, tiled=...  28.9 us
    scatter-add x10, other arithmetic, on_device(): grad_table = grad_table.at[index_two[sample]].add(back_agg)  28.4 us
    all_to_all x1, waiting for transfers between devices, on_device(): lax.all_to_all(outgoing, 'feat', split_axis=0, concat_axis=0, tiled=True)  27.5 us
    all_to_all x1, waiting for transfers between devices, on_device(): lax.all_to_all(grad_table[node_count:].reshape(feat_devs, capacity, hidde...  26.6 us
    all_to_all x1, waiting for transfers between devices, on_device(): lax.all_to_all(outgoing_one, 'feat', split_axis=0, concat_axis=0, tiled=T...  14.8 us
    psum x1, blocking collectives, on_device(): reduced = lax.psum(jnp.sum(incoming_grad, axis=0), 'rep')  13.3 us
    all_to_all x1, starting transfers between devices, on_device(): lax.all_to_all(outgoing_one, 'feat', split_axis=0, concat_axis=0, tiled=T...  13 us
  transfers between devices with their start and end apart: 3, of which 3 were waited for; matrix products, arithmetic and copies ran while one was open for 1% of the time, Pallas kernels for 0%

profile of v1, /device:TPU:1, one launch (start us, length us, event | category | flops | bytes accessed | tf_op | source)
XLA Modules:
  0.0 272.6 jit_solution(2051034119500823161)
XLA Ops:
  0.7 0.9 slice.236
  1.6 0.9 copy.43
  2.6 0.8 broadcast_in_dim.30
  3.5 1.2 pad_maximum_fusion.3
  4.7 13.0 %all-to-all-start = ((bf16[64,2,1792]{2,1,0:T(2,128)(2,1)}), bf16[64,2,1792]{2,1,0:T(2,128)(2,1)S(1)}, u32[]{:S(2)}, u32[]{:S(2)}) async-start(bf16[64,2,1792]{2,1,0:T(2,128)(2,1)} %pad_maximum_fusion.3), calls=%async_computation | async-start | bytes 917504 | tf_op jit(solution)/shard_map/all_to_all | solution.py:46
  17.9 0.7 dynamic-slice_subtract_fusion
  18.7 14.8 %all-to-all-done = bf16[64,2,1792]{2,1,0:T(2,128)(2,1)S(1)} async-done(((bf16[64,2,1792]{2,1,0:T(2,128)(2,1)}), bf16[64,2,1792]{2,1,0:T(2,128)(2,1)S(1)}, u32[]{:S(2)}, u32[]{:S(2)}) %all-to-all-start) | async-done | bytes 458784 | tf_op jit(solution)/shard_map/all_to_all | solution.py:46
  34.1 2.2 fusion.2
  36.4 1.0 fusion.18
  37.4 7.5 %gather_fusion = bf16[2048,256]{1,0:T(8,128)(2,1)S(1)} fusion(bf16[256,256]{1,0:T(8,128)(2,1)S(1)} %get-tuple-element.42, s32[2048]{0:T(1024)S(1)} %broadcast_clamp_fusion), kind=kCustom, calls=%fused_computation | custom fusion | bytes 2105344 | tf_op jit(solution)/shard_map/gather | solution.py:73
  44.9 1.3 broadcast_select_fusion
  46.1 6.6 %all-to-all-start.1 = ((bf16[64,32,256]{2,1,0:T(8,128)(2,1)}), bf16[64,32,256]{2,1,0:T(8,128)(2,1)S(1)}, u32[]{:S(2)}, u32[]{:S(2)}) async-start(bf16[64,32,256]{2,1,0:T(8,128)(2,1)} %broadcast_select_fusion), calls=%async_computation.1 | async-start | bytes 2097152 | tf_op jit(solution)/shard_map/all_to_all | solution.py:75
  53.6 27.5 %all-to-all-done.1 = bf16[64,32,256]{2,1,0:T(8,128)(2,1)S(1)} async-done(((bf16[64,32,256]{2,1,0:T(8,128)(2,1)}), bf16[64,32,256]{2,1,0:T(8,128)(2,1)S(1)}, u32[]{:S(2)}, u32[]{:S(2)}) %all-to-all-start.1) | async-done | bytes 1048608 | tf_op jit(solution)/shard_map/all_to_all | solution.py:75
  81.2 1.2 gather_fusion.10
  82.3 1.2 gather_fusion.9
  83.6 1.2 gather_fusion.8
  84.7 1.2 gather_fusion.7
  85.9 1.2 gather_fusion.6
  87.0 1.2 gather_fusion.5
  88.2 1.2 gather_fusion.4
  89.4 1.2 gather_fusion.3
  90.5 1.2 gather_fusion.2
  91.7 1.2 gather_fusion.1
  93.0 1.0 fusion.24
  94.2 2.7 scatter_custom_fusion
  96.9 3.0 %scatter_fusion = f32[2304,256]{1,0:T(8,128)S(1)} fusion(f32[2304,256]{1,0:T(8,128)S(1)} %scatter_custom_fusion, s32[256]{0:T(256)} %bitcast.147, f32[256,256]{1,0:T(8,128)S(1)} %convolution_multiply_fusion), kind=kCustom, calls=%fused_computation.12 | custom fusion | flops 65536 | bytes 787456 | tf_op jit(solution)/shard_map/scatter-add | solution.py:109
  99.9 2.8 %scatter_fusion.1 = f32[2304,256]{1,0:T(8,128)S(1)} fusion(f32[2304,256]{1,0:T(8,128)S(1)} %scatter_fusion, s32[256]{0:T(256)S(1)} %bitcast.145, f32[256,256]{1,0:T(8,128)S(1)} %convolution_multiply_fusion), kind=kCustom, calls=%fused_computation.13 | custom fusion | flops 65536 | bytes 787456 | tf_op jit(solution)/shard_map/scatter-add | solution.py:109
  102.7 3.0 %scatter_fusion.2 = f32[2304,256]{1,0:T(8,128)S(1)} fusion(f32[2304,256]{1,0:T(8,128)S(1)} %scatter_fusion.1, s32[256]{0:T(256)S(1)} %bitcast.143, f32[256,256]{1,0:T(8,128)S(1)} %convolution_multiply_fusion), kind=kCustom, calls=%fused_computation.14 | custom fusion | flops 65536 | bytes 787456 | tf_op jit(solution)/shard_map/scatter-add | solution.py:109
  105.8 2.8 %scatter_fusion.3 = f32[2304,256]{1,0:T(8,128)S(1)} fusion(f32[2304,256]{1,0:T(8,128)S(1)} %scatter_fusion.2, s32[256]{0:T(256)S(1)} %bitcast.141, f32[256,256]{1,0:T(8,128)S(1)} %convolution_multiply_fusion), kind=kCustom, calls=%fused_computation.15 | custom fusion | flops 65536 | bytes 787456 | tf_op jit(solution)/shard_map/scatter-add | solution.py:109
  108.6 2.8 %scatter_fusion.4 = f32[2304,256]{1,0:T(8,128)S(1)} fusion(f32[2304,256]{1,0:T(8,128)S(1)} %scatter_fusion.3, s32[256]{0:T(256)S(1)} %bitcast.139, f32[256,256]{1,0:T(8,128)S(1)} %convolution_multiply_fusion), kind=kCustom, calls=%fused_computation.16 | custom fusion | flops 65536 | bytes 787456 | tf_op jit(solution)/shard_map/scatter-add | solution.py:109
  111.5 2.8 %scatter_fusion.5 = f32[2304,256]{1,0:T(8,128)S(1)} fusion(f32[2304,256]{1,0:T(8,128)S(1)} %scatter_fusion.4, s32[256]{0:T(256)S(1)} %bitcast.137, f32[256,256]{1,0:T(8,128)S(1)} %convolution_multiply_fusion), kind=kCustom, calls=%fused_computation.17 | custom fusion | flops 65536 | bytes 787456 | tf_op jit(solution)/shard_map/scatter-add | solution.py:109
  114.3 2.8 %scatter_fusion.6 = f32[2304,256]{1,0:T(8,128)S(1)} fusion(f32[2304,256]{1,0:T(8,128)S(1)} %scatter_fusion.5, s32[256]{0:T(256)S(1)} %bitcast.135, f32[256,256]{1,0:T(8,128)S(1)} %convolution_multiply_fusion), kind=kCustom, calls=%fused_computation.18 | custom fusion | flops 65536 | bytes 787456 | tf_op jit(solution)/shard_map/scatter-add | solution.py:109
  117.2 2.8 %scatter_fusion.7 = f32[2304,256]{1,0:T(8,128)S(1)} fusion(f32[2304,256]{1,0:T(8,128)S(1)} %scatter_fusion.6, s32[256]{0:T(256)S(1)} %bitcast.133, f32[256,256]{1,0:T(8,128)S(1)} %convolution_multiply_fusion), kind=kCustom, calls=%fused_computation.19 | custom fusion | flops 65536 | bytes 787456 | tf_op jit(solution)/shard_map/scatter-add | solution.py:109
  120.0 2.8 %scatter_fusion.8 = f32[2304,256]{1,0:T(8,128)S(1)} fusion(f32[2304,256]{1,0:T(8,128)S(1)} %scatter_fusion.7, s32[256]{0:T(256)S(1)} %bitcast.131, f32[256,256]{1,0:T(8,128)S(1)} %convolution_multiply_fusion), kind=kCustom, calls=%fused_computation.20 | custom fusion | flops 65536 | bytes 787456 | tf_op jit(solution)/shard_map/scatter-add | solution.py:109
  122.8 1.1 slice.299
  124.0 6.4 %all-to-all-start.2 = ((bf16[64,32,256]{2,1,0:T(8,128)(2,1)}), bf16[64,32,256]{2,1,0:T(8,128)(2,1)}, u32[]{:S(2)}, u32[]{:S(2)}) async-start(bf16[64,32,256]{2,1,0:T(8,128)(2,1)} %bitcast.53), calls=%async_computation.2 | async-start | bytes 2097152 | tf_op jit(solution)/shard_map/all_to_all | solution.py:111
  131.0 1.2 convolution_add_fusion
  132.2 26.6 %all-to-all-done.2 = bf16[64,32,256]{2,1,0:T(8,128)(2,1)} async-done(((bf16[64,32,256]{2,1,0:T(8,128)(2,1)}), bf16[64,32,256]{2,1,0:T(8,128)(2,1)}, u32[]{:S(2)}, u32[]{:S(2)}) %all-to-all-start.2) | async-done | bytes 1048608 | tf_op jit(solution)/shard_map/all_to_all | solution.py:111
  158.8 1.6 convert_select_fusion
  160.4 11.9 %scatter_fusion.9 = f32[256,256]{1,0:T(8,128)S(1)} fusion(f32[256,256]{1,0:T(8,128)S(1)} %convolution_add_fusion, s32[2048]{0:T(1024)S(1)} %reshape.486, f32[2048,256]{1,0:T(8,128)S(1)} %bitcast.118), kind=kCustom, calls=%fused_computation.21 | custom fusion | flops 524288 | bytes 6299648 | tf_op jit(solution)/shard_map/scatter-add | solution.py:119
  172.4 1.0 fusion.37
  174.2 0.5 all_to_all.18
  174.7 28.9 %all_to_all.24 = f32[64,1,3072]{2,1,0:T(1,128)S(1)} all-to-all(f32[64,1,3072]{2,1,0:T(1,128)S(1)} %all_to_all.18), channel_id=1, replica_groups=mesh['feat'=64,'rep'=4] {'feat'}, dimensions={0} | all-to-all | bytes 1572864 | tf_op jit(solution)/shard_map/all_to_all | solution.py:133
  203.6 0.5 reduce_sum.9
  204.1 13.3 %psum.7 = f32[3072]{0:T(1024)S(1)} all-reduce(f32[3072]{0:T(1024)S(1)} %reduce_sum.9), channel_id=1, replica_groups=mesh['feat'=64,'rep'=4] {'rep'}, use_global_device_ids=true, to_apply=%region_12.13 | all-reduce | flops 3072 | bytes 24576 | tf_op jit(solution)/shard_map/psum | solution.py:134
  217.5 0.6 slice.212
  218.1 53.1 %all_gather.3 = f32[131072]{0:T(1024)S(1)} all-gather(f32[2048]{0:T(1024)S(1)} %slice.260), channel_id=1, replica_groups=mesh['feat'=64,'rep'=4] {'feat'}, dimensions={0}, use_global_device_ids=true | all-gather | bytes 532480 | tf_op jit(solution)/shard_map/all_gather | solution.py:137
  271.2 0.9 reshape.482
  (96 shorter events, 3.6 us)
Async XLA Ops:
  0.6 17.1 %copy-start.6 = (s32[1,1,64,32]{2,3,1,0:T(8,128)S(1)}, s32[1,1,64,32]{2,3,1,0:T(8,128)}, u32[]{:S(2)}) copy-start(s32[1,1,64,32]{2,3,1,0:T(8,128)} %param.14) | copy-start | bytes 24580
  0.6 18.0 %copy-start.26 = (s32[1,1,64]{2,1,0:T(1,128)S(1)}, s32[1,1,64]{2,1,0:T(1,128)}, u32[]{:S(2)}) copy-start(s32[1,1,64]{2,1,0:T(1,128)} %param.15) | copy-start | bytes 772
  4.7 28.9 %all-to-all-start = ((bf16[64,2,1792]{2,1,0:T(2,128)(2,1)}), bf16[64,2,1792]{2,1,0:T(2,128)(2,1)S(1)}, u32[]{:S(2)}, u32[]{:S(2)}) async-start(bf16[64,2,1792]{2,1,0:T(2,128)(2,1)} %pad_maximum_fusion.3), calls=%async_computation | async-start | bytes 917504 | tf_op jit(solution)/shard_map/all_to_all | solution.py:46
  33.8 2.6 copy-start.1
  36.3 1.0 copy-start.4
  44.9 7.9 %copy-start.7 = (s32[1,10,256]{2,0,1:T(1,128)S(1)}, s32[1,10,256]{2,0,1:T(1,128)}, u32[]{:S(2)}) copy-start(s32[1,10,256]{2,0,1:T(1,128)} %param.16) | copy-start | bytes 30724
  44.9 8.5 %copy-start.3 = (bf16[2,256,256]{2,1,0:T(8,128)(2,1)S(1)}, bf16[2,256,256]{2,1,0:T(8,128)(2,1)}, u32[]{:S(2)}) copy-start(bf16[2,256,256]{2,1,0:T(8,128)(2,1)} %param.13) | copy-start | bytes 786436
  46.1 35.0 %all-to-all-start.1 = ((bf16[64,32,256]{2,1,0:T(8,128)(2,1)}), bf16[64,32,256]{2,1,0:T(8,128)(2,1)S(1)}, u32[]{:S(2)}, u32[]{:S(2)}) async-start(bf16[64,32,256]{2,1,0:T(8,128)(2,1)} %broadcast_select_fusion), calls=%async_computation.1 | async-start | bytes 2097152 | tf_op jit(solution)/shard_map/all_to_all | solution.py:75
  52.8 0.6 copy-start.25
  52.8 30.7 %copy-start.8 = (s32[256,1]{0,1:T(1,128)}, s32[256,1]{0,1:T(1,128)S(1)}, u32[]{:S(2)}) copy-start(s32[256,1]{0,1:T(1,128)S(1)} %get-tuple-element.40) | copy-start | bytes 3076
  52.8 30.7 %copy-start.10 = (s32[256,1]{0,1:T(1,128)}, s32[256,1]{0,1:T(1,128)S(1)}, u32[]{:S(2)}) copy-start(s32[256,1]{0,1:T(1,128)S(1)} %get-tuple-element.41) | copy-start | bytes 3076
  52.8 30.7 %copy-start.12 = (s32[256,1]{0,1:T(1,128)}, s32[256,1]{0,1:T(1,128)S(1)}, u32[]{:S(2)}) copy-start(s32[256,1]{0,1:T(1,128)S(1)} %get-tuple-element.33) | copy-start | bytes 3076
  52.8 30.7 %copy-start.14 = (s32[256,1]{0,1:T(1,128)}, s32[256,1]{0,1:T(1,128)S(1)}, u32[]{:S(2)}) copy-start(s32[256,1]{0,1:T(1,128)S(1)} %get-tuple-element.34) | copy-start | bytes 3076
  52.8 30.7 %copy-start.16 = (s32[256,1]{0,1:T(1,128)}, s32[256,1]{0,1:T(1,128)S(1)}, u32[]{:S(2)}) copy-start(s32[256,1]{0,1:T(1,128)S(1)} %get-tuple-element.35) | copy-start | bytes 3076
  52.8 30.7 %copy-start.18 = (s32[256,1]{0,1:T(1,128)}, s32[256,1]{0,1:T(1,128)S(1)}, u32[]{:S(2)}) copy-start(s32[256,1]{0,1:T(1,128)S(1)} %get-tuple-element.36) | copy-start | bytes 3076
  52.8 30.7 %copy-start.20 = (s32[256,1]{0,1:T(1,128)}, s32[256,1]{0,1:T(1,128)S(1)}, u32[]{:S(2)}) copy-start(s32[256,1]{0,1:T(1,128)S(1)} %get-tuple-element.37) | copy-start | bytes 3076
  52.8 30.7 %copy-start.22 = (s32[256,1]{0,1:T(1,128)}, s32[256,1]{0,1:T(1,128)S(1)}, u32[]{:S(2)}) copy-start(s32[256,1]{0,1:T(1,128)S(1)} %get-tuple-element.38) | copy-start | bytes 3076
  52.8 30.7 %copy-start.24 = (s32[256,1]{0,1:T(1,128)}, s32[256,1]{0,1:T(1,128)S(1)}, u32[]{:S(2)}) copy-start(s32[256,1]{0,1:T(1,128)S(1)} %get-tuple-element.39) | copy-start | bytes 3076
  89.3 3.7 %copy-start.27 = (bf16[1,256,256]{2,1,0:T(8,128)(2,1)S(1)}, bf16[1,256,256]{2,1,0:T(8,128)(2,1)}, u32[]{:S(2)}) copy-start(bf16[1,256,256]{2,1,0:T(8,128)(2,1)} %param.17) | copy-start | bytes 393220
  94.0 36.6 %copy-start = (bf16[256,256]{1,0:T(8,128)(2,1)}, bf16[256,256]{1,0:T(8,128)(2,1)S(1)}, u32[]{:S(2)}) copy-start(bf16[256,256]{1,0:T(8,128)(2,1)S(1)} %get-tuple-element.15) | copy-start | bytes 393220
  96.9 3.0 %copy-start.23 = (s32[256,1]{0,1:T(1,128)S(1)}, s32[256,1]{0,1:T(1,128)}, u32[]{:S(2)}) copy-start(s32[256,1]{0,1:T(1,128)} %copy-done.22) | copy-start | bytes 3076
  99.8 2.8 %copy-start.21 = (s32[256,1]{0,1:T(1,128)S(1)}, s32[256,1]{0,1:T(1,128)}, u32[]{:S(2)}) copy-start(s32[256,1]{0,1:T(1,128)} %copy-done.20) | copy-start | bytes 3076
  102.7 3.1 %copy-start.19 = (s32[256,1]{0,1:T(1,128)S(1)}, s32[256,1]{0,1:T(1,128)}, u32[]{:S(2)}) copy-start(s32[256,1]{0,1:T(1,128)} %copy-done.18) | copy-start | bytes 3076
  105.8 2.8 %copy-start.17 = (s32[256,1]{0,1:T(1,128)S(1)}, s32[256,1]{0,1:T(1,128)}, u32[]{:S(2)}) copy-start(s32[256,1]{0,1:T(1,128)} %copy-done.16) | copy-start | bytes 3076
  108.6 2.8 %copy-start.15 = (s32[256,1]{0,1:T(1,128)S(1)}, s32[256,1]{0,1:T(1,128)}, u32[]{:S(2)}) copy-start(s32[256,1]{0,1:T(1,128)} %copy-done.14) | copy-start | bytes 3076
  111.5 2.8 %copy-start.13 = (s32[256,1]{0,1:T(1,128)S(1)}, s32[256,1]{0,1:T(1,128)}, u32[]{:S(2)}) copy-start(s32[256,1]{0,1:T(1,128)} %copy-done.12) | copy-start | bytes 3076
  114.3 2.8 %copy-start.11 = (s32[256,1]{0,1:T(1,128)S(1)}, s32[256,1]{0,1:T(1,128)}, u32[]{:S(2)}) copy-start(s32[256,1]{0,1:T(1,128)} %copy-done.10) | copy-start | bytes 3076
  117.2 2.8 %copy-start.9 = (s32[256,1]{0,1:T(1,128)S(1)}, s32[256,1]{0,1:T(1,128)}, u32[]{:S(2)}) copy-start(s32[256,1]{0,1:T(1,128)} %copy-done.8) | copy-start | bytes 3076
  124.0 34.8 %all-to-all-start.2 = ((bf16[64,32,256]{2,1,0:T(8,128)(2,1)}), bf16[64,32,256]{2,1,0:T(8,128)(2,1)}, u32[]{:S(2)}, u32[]{:S(2)}) async-start(bf16[64,32,256]{2,1,0:T(8,128)(2,1)} %bitcast.53), calls=%async_computation.2 | async-start | bytes 2097152 | tf_op jit(solution)/shard_map/all_to_all | solution.py:111
  160.4 12.0 %copy-start.2 = (f32[256,256]{1,0:T(8,128)S(1)}, f32[256,256]{1,0:T(8,128)}, u32[]{:S(2)}) copy-start(f32[256,256]{1,0:T(8,128)} %get-tuple-element.43) | copy-start | bytes 786436
  160.4 13.0 %copy-start.5 = (bf16[128,256]{1,0:T(8,128)(2,1)S(1)}, bf16[128,256]{1,0:T(8,128)(2,1)}, u32[]{:S(2)}) copy-start(bf16[128,256]{1,0:T(8,128)(2,1)} %copy-done.4) | copy-start | bytes 196612

commit v2 on v1

--- a/solution.py
+++ b/solution.py
@@ -67,21 +67,31 @@
 
     send_slots = send_rows[0, 0]
     counts = halo_count[0, 0]
-    capacity = send_slots.shape[1]
+    peers, capacity = send_slots.shape
     live_slots = lax.broadcasted_iota(jnp.int32, send_slots.shape, 1) < counts[:, None]
-    outgoing = jnp.where(
-        live_slots[:, :, None], hidden_one[send_slots], jnp.zeros((), jnp.bfloat16)
+    local_rows = lax.broadcasted_iota(jnp.int32, (peers, capacity, node_count), 2)
+    picks = ((send_slots[:, :, None] == local_rows) & live_slots[:, :, None]).astype(jnp.bfloat16)
+    picks = picks.reshape(peers * capacity, node_count)
+    outgoing = jnp.einsum(
+        "ji,ih->jh", picks, hidden_one, preferred_element_type=jnp.float32
+    ).astype(jnp.bfloat16)
+    incoming = lax.all_to_all(
+        outgoing.reshape(peers, capacity, hidden_width), "feat", split_axis=0, concat_axis=0, tiled=True
     )
-    incoming = lax.all_to_all(outgoing, "feat", split_axis=0, concat_axis=0, tiled=True)
     table_two = jnp.concatenate(
         [hidden_one, incoming.reshape(feat_devs * capacity, hidden_width)], axis=0
     )
     index_two = neighbors_two[0]
     fanout_two = index_two.shape[0]
     seed_rows = index_two.shape[1]
-    summed_two = jnp.zeros((seed_rows, hidden_width), jnp.float32)
+    table_rows = table_two.shape[0]
+    rows_two = lax.broadcasted_iota(jnp.int32, (seed_rows, table_rows), 1)
+    tallies_two = jnp.zeros((seed_rows, table_rows), jnp.float32)
     for sample in range(fanout_two):
-        summed_two = summed_two + table_two[index_two[sample]].astype(jnp.float32)
+        tallies_two = tallies_two + (index_two[sample][:, None] == rows_two).astype(jnp.float32)
+    summed_two = jnp.einsum(
+        "dr,rh->dh", tallies_two.astype(jnp.bfloat16), table_two, preferred_element_type=jnp.float32
+    )
     aggregate_two = (summed_two / fanout_two).astype(jnp.bfloat16)
     pre_two = jnp.dot(hidden_one, weight_two[0], preferred_element_type=jnp.float32) + jnp.dot(
         aggregate_two, weight_two[1], preferred_element_type=jnp.float32
@@ -104,19 +114,21 @@
         jnp.einsum("rk,hk->rh", slope_two, weight_two[1], preferred_element_type=jnp.float32)
         / fanout_two
     )
-    grad_table = jnp.zeros((table_two.shape[0], hidden_width), jnp.float32)
-    for sample in range(fanout_two):
-        grad_table = grad_table.at[index_two[sample]].add(back_agg)
-    grad_table = grad_table.at[:seed_rows].add(back_self)
+    grad_table = jnp.einsum(
+        "dr,dh->rh", tallies_two, back_agg, precision=lax.Precision.HIGHEST,
+        preferred_element_type=jnp.float32,
+    )
     returned = lax.all_to_all(
-        grad_table[node_count:].reshape(feat_devs, capacity, hidden_width).astype(jnp.bfloat16),
+        grad_table[node_count:].reshape(peers, capacity, hidden_width).astype(jnp.bfloat16),
         "feat",
         split_axis=0,
         concat_axis=0,
         tiled=True,
-    ).astype(jnp.float32)
-    returned = jnp.where(live_slots[:, :, None], returned, 0.0)
-    back_one = grad_table[:node_count].at[send_slots].add(returned)
+    )
+    back_one = grad_table[:node_count] + back_self + jnp.einsum(
+        "ji,jh->ih", picks, returned.reshape(peers * capacity, hidden_width),
+        preferred_element_type=jnp.float32,
+    )
     slope_one = (back_one * elu_slope(pre_one)).astype(jnp.bfloat16)
     local_one = jnp.stack(
         [
@@ -131,12 +143,18 @@
     two_part = local_two.reshape(feat_devs, -1)
     outgoing_grad = jnp.concatenate([one_part, two_part], axis=1)
     incoming_grad = lax.all_to_all(outgoing_grad, "feat", split_axis=0, concat_axis=0, tiled=True)
-    reduced = lax.psum(jnp.sum(incoming_grad, axis=0), "rep")
+    feat_summed = jnp.sum(incoming_grad, axis=0)
+    rep_copies = jnp.broadcast_to(feat_summed[None], (rep_devs,) + feat_summed.shape)
+    reduced = jnp.sum(
+        lax.all_to_all(rep_copies, "rep", split_axis=0, concat_axis=0, tiled=True), axis=0
+    )
     one_size = one_part.shape[1]
     grad_one = reduced[:one_size].reshape(2, cols_dev, hidden_width)
-    grad_two = lax.all_gather(reduced[one_size:], "feat", axis=0, tiled=True).reshape(
-        local_two.shape
-    )
+    two_piece = reduced[one_size:]
+    two_copies = jnp.broadcast_to(two_piece[None], (feat_devs,) + two_piece.shape)
+    grad_two = lax.all_to_all(
+        two_copies, "feat", split_axis=0, concat_axis=0, tiled=True
+    ).reshape(local_two.shape)
     return (hidden_two[None], grad_one, grad_two)
 
 

time: 278 us -> 193 us (0.69); the launches traced: 273 us -> 192 us
  blocking collectives: 95.4 us -> 37.3 us
  other arithmetic: 46.2 us -> 3.96 us
  waiting for transfers between devices: 69 us -> 87.6 us
  local copies, waits for them, and re-layouts: 26.5 us -> 9.58 us
  matrix products: 7.54 us -> 19.9 us
  starting transfers between devices: 25.9 us -> 33.1 us
    all_gather x1 -> x0, blocking collectives: 53.1 us -> none  [on_device(): lax.all_gather(reduced[one_size:], 'feat', axis=0, tiled=True)]
    scatter-add x11 -> x0, other arithmetic: 40.3 us -> none  [the longest x10 28.4 us: on_device(): grad_table = grad_table.at[index_two[sample]].add(back_agg)]
    gather x11 -> x0, local copies, waits for them, and re-layouts: 19 us -> none  [the longest x10 11.5 us: on_device(): summed_two = summed_two + table_two[index_two[sample]].astype(jnp.float32)]
    all_to_all x2 -> x3, waiting for transfers between devices: 54.2 us -> 72.8 us  [the longest x1 28.3 us: on_device(): lax.all_to_all(outgoing.reshape(peers, capacity, hidden_width), 'feat', s...]
    dot_general x0 -> x4, matrix products: none -> 13.9 us  [the longest x1 6.53 us: on_device(): jnp.einsum('dr,dh->rh', tallies_two, back_agg, precision=lax.Precision.HI...]
    psum x1 -> x0, blocking collectives: 13.3 us -> none  [on_device(): reduced = lax.psum(jnp.sum(incoming_grad, axis=0), 'rep')]
    all_to_all x0 -> x1, blocking collectives: none -> 8.37 us  [on_device(): lax.all_to_all(rep_copies, 'rep', split_axis=0, concat_axis=0, tiled=True)]
    all_to_all x2 -> x3, starting transfers between devices: 13 us -> 20.2 us  [the longest x1 7.65 us: on_device(): lax.all_to_all(two_copies, 'feat', split_axis=0, concat_axis=0, tiled=True)]
  transfers between devices with their start and end apart: 3 -> 4, of which waited for: 3 -> 4; matrix products, arithmetic and copies ran while one was open for 1% -> 1% of each run, Pallas kernels for 0% -> 0%
where the time goes in v2:
time: 193 us; the launch traced here: 192 us
  waiting for transfers between devices  87.6 us (45%)
  blocking collectives  37.3 us (19%)
  starting transfers between devices  33.1 us (17%)
  matrix products  19.9 us (10%)
  local copies, waits for them, and re-layouts  9.58 us (5%)
  other arithmetic  3.96 us (2%)
    all_to_all x1, blocking collectives, on_device(): lax.all_to_all(outgoing_grad, 'feat', split_axis=0, concat_axis=0, tiled=...  28.9 us
    all_to_all x1, waiting for transfers between devices, on_device(): lax.all_to_all(outgoing.reshape(peers, capacity, hidden_width), 'feat', s...  28.3 us
    all_to_all x1, waiting for transfers between devices, on_device(): lax.all_to_all(grad_table[node_count:].reshape(peers, capacity, hidden_wi...  27.8 us
    all_to_all x1, waiting for transfers between devices, on_device(): lax.all_to_all(two_copies, 'feat', split_axis=0, concat_axis=0, tiled=True)  16.7 us
    all_to_all x1, waiting for transfers between devices, on_device(): lax.all_to_all(outgoing_one, 'feat', split_axis=0, concat_axis=0, tiled=T...  14.8 us
    all_to_all x1, starting transfers between devices, on_device(): lax.all_to_all(outgoing_one, 'feat', split_axis=0, concat_axis=0, tiled=T...  13 us
    all_to_all x1, blocking collectives, on_device(): lax.all_to_all(rep_copies, 'rep', split_axis=0, concat_axis=0, tiled=True)  8.37 us
    all_to_all x1, starting transfers between devices, on_device(): lax.all_to_all(two_copies, 'feat', split_axis=0, concat_axis=0, tiled=True)  7.65 us
  transfers between devices with their start and end apart: 4, of which 4 were waited for; matrix products, arithmetic and copies ran while one was open for 1% of the time, Pallas kernels for 0%

profile of v2, /device:TPU:1, one launch (start us, length us, event | category | flops | bytes accessed | tf_op | source)
XLA Modules:
  0.0 192.4 jit_solution(341202582496497474)
XLA Ops:
  0.7 0.9 copy.78
  1.6 0.1 copy.60
  1.7 0.9 slice.187
  2.6 0.1 broadcast_in_dim.12
  2.8 0.8 broadcast_in_dim.28
  3.5 1.2 pad_maximum_fusion.2
  4.7 13.0 %all-to-all-start = ((bf16[64,2,1792]{2,1,0:T(2,128)(2,1)}), bf16[64,2,1792]{2,1,0:T(2,128)(2,1)S(1)}, u32[]{:S(2)}, u32[]{:S(2)}) async-start(bf16[64,2,1792]{2,1,0:T(2,128)(2,1)} %pad_maximum_fusion.2), calls=%async_computation | async-start | bytes 917504 | tf_op jit(solution)/shard_map/all_to_all | solution.py:46
  17.8 0.1 lt.25
  17.9 0.1 copy.65
  18.0 0.7 dynamic-slice_subtract_fusion
  18.8 14.8 %all-to-all-done = bf16[64,2,1792]{2,1,0:T(2,128)(2,1)S(1)} async-done(((bf16[64,2,1792]{2,1,0:T(2,128)(2,1)}), bf16[64,2,1792]{2,1,0:T(2,128)(2,1)S(1)}, u32[]{:S(2)}, u32[]{:S(2)}) %all-to-all-start) | async-done | bytes 458784 | tf_op jit(solution)/shard_map/all_to_all | solution.py:46
  33.6 0.2 reshape.180
  33.8 0.1 copy.62
  33.9 0.2 fusion.64
  34.1 2.2 %fusion.27 = bf16[128,256]{1,0:T(8,128)(2,1)S(1)} fusion(s32[256]{0:T(256)S(1)} %bitcast.113, s32[256]{0:T(256)S(1)} %bitcast.114, s32[256]{0:T(256)S(1)} %bitcast.115, s32[256]{0:T(256)S(1)} %bitcast.116, s32[256]{0:T(256)S(1)} %bitcast.117, s32[256]{0:T(256)S(1)} %bitcast.118, s32[256]{0:T(256)S(1)} %bitcast.119, s32[256]{0:T(256)S(1)} %bitcast.120, ...), kind=kOutput, calls=%fused_computation.37 | convolution fusion | flops 78970880 | bytes 343040 | tf_op jit(solution)/shard_map/fs,vs->fv/dot_general | solution.py:60
  36.3 0.3 fusion.48
  36.6 2.6 %convolution_convert_fusion = bf16[2048,256]{1,0:T(8,128)(2,1)} fusion(bf16[256,256]{1,0:T(8,128)(2,1)S(1)} %get-tuple-element.30, s32[2048]{0:T(1024)S(1)} %eq.342, pred[2048]{0:T(1024)(128)(4,1)S(1)} %lt.25), kind=kOutput, calls=%fused_computation | convolution fusion | flops 270008320 | bytes 1189888 | tf_op jit(solution)/shard_map/ji,ih->jh/dot_general | solution.py:75
  39.3 6.3 %all-to-all-start.1 = ((bf16[64,32,256]{2,1,0:T(8,128)(2,1)}), bf16[64,32,256]{2,1,0:T(8,128)(2,1)S(1)}, u32[]{:S(2)}, u32[]{:S(2)}) async-start(bf16[64,32,256]{2,1,0:T(8,128)(2,1)} %bitcast.37), calls=%async_computation.1 | async-start | bytes 2097152 | tf_op jit(solution)/shard_map/all_to_all | solution.py:78
  45.6 0.2 fusion.58
  45.8 28.3 %all-to-all-done.1 = bf16[64,32,256]{2,1,0:T(8,128)(2,1)S(1)} async-done(((bf16[64,32,256]{2,1,0:T(8,128)(2,1)}), bf16[64,32,256]{2,1,0:T(8,128)(2,1)S(1)}, u32[]{:S(2)}, u32[]{:S(2)}) %all-to-all-start.1) | async-done | bytes 1048608 | tf_op jit(solution)/shard_map/all_to_all | solution.py:78
  74.1 3.2 %fusion.21 = bf16[256,256]{1,0:T(8,128)(2,1)S(1)} fusion(bf16[2048,256]{1,0:T(8,128)(2,1)S(1)} %bitcast.101, bf16[256,256]{1,0:T(8,128)(2,1)S(1)} %get-tuple-element.30, s32[256]{0:T(256)S(1)} %bitcast.143, s32[256]{0:T(256)S(1)} %bitcast.145, s32[256]{0:T(256)S(1)} %bitcast.129, s32[256]{0:T(256)S(1)} %bitcast.131, s32[256]{0:T(256)S(1)} %bitcast.133, ...), kind=kOutput, calls=%fused_computation.34 | convolution fusion | flops 322174976 | bytes 1320960 | tf_op jit(solution)/shard_map/dr,rh->dh/dot_general | solution.py:92
  77.3 1.0 fusion.52
  78.2 0.2 convolution_multiply_fusion
  78.5 6.5 %fusion.10 = f32[2304,256]{1,0:T(8,128)S(1)} fusion(f32[256,256]{1,0:T(8,128)S(1)} %convolution_multiply_fusion, s32[256]{0:T(256)S(1)} %bitcast.144, s32[256]{0:T(256)S(1)} %bitcast.146, s32[256]{0:T(256)S(1)} %bitcast.130, s32[256]{0:T(256)S(1)} %bitcast.132, s32[256]{0:T(256)S(1)} %bitcast.134, s32[256]{0:T(256)S(1)} %bitcast.136, s32[256]{0:T(256)S(1)} %bitcast.138, ...), kind=kOutput, calls=%fused_computation.23 | convolution fusion | flops 1829044224 | bytes 2631680 | tf_op jit(solution)/shard_map/dr,dh->rh/dot_general | solution.py:117
  85.0 1.4 copy-done
  86.4 1.1 slice.240
  87.5 6.2 %all-to-all-start.2 = ((bf16[64,32,256]{2,1,0:T(8,128)(2,1)}), bf16[64,32,256]{2,1,0:T(8,128)(2,1)S(1)}, u32[]{:S(2)}, u32[]{:S(2)}) async-start(bf16[64,32,256]{2,1,0:T(8,128)(2,1)} %bitcast.43), calls=%async_computation.2 | async-start | bytes 2097152 | tf_op jit(solution)/shard_map/all_to_all | solution.py:121
  93.7 0.1 copy.66
  93.8 0.2 convolution_bitcast_fusion.1
  94.0 0.2 convolution_bitcast_fusion
  94.3 0.1 reshape.185
  94.4 27.8 %all-to-all-done.2 = bf16[64,32,256]{2,1,0:T(8,128)(2,1)S(1)} async-done(((bf16[64,32,256]{2,1,0:T(8,128)(2,1)}), bf16[64,32,256]{2,1,0:T(8,128)(2,1)S(1)}, u32[]{:S(2)}, u32[]{:S(2)}) %all-to-all-start.2) | async-done | bytes 1048608 | tf_op jit(solution)/shard_map/all_to_all | solution.py:121
  122.2 1.5 fusion.13
  123.8 1.2 fusion.26
  125.0 0.2 fusion.65
  125.1 0.2 fusion.73
  125.5 0.1 maximum_bitcast_fusion
  125.6 0.2 reshape.184
  125.9 0.5 all_to_all.26
  126.4 28.9 %all_to_all.36 = f32[64,1,3072]{2,1,0:T(1,128)S(1)} all-to-all(f32[64,1,3072]{2,1,0:T(1,128)S(1)} %all_to_all.26), channel_id=1, replica_groups=mesh['feat'=64,'rep'=4] {'feat'}, dimensions={0} | all-to-all | bytes 1572864 | tf_op jit(solution)/shard_map/all_to_all | solution.py:145
  155.3 0.5 reduce_sum.18
  155.8 8.4 %all_to_all.37 = f32[4,1,3072]{2,1,0:T(1,128)S(1)} all-to-all(f32[4,1,3072]{2,1,0:T(1,128)S(1)} %broadcast_in_dim.30), channel_id=1, replica_groups=mesh['feat'=64,'rep'=4] {'rep'}, dimensions={0} | all-to-all | bytes 98304 | tf_op jit(solution)/shard_map/all_to_all | solution.py:149
  164.3 1.1 broadcast_in_dim.31
  165.3 7.7 %all-to-all-start.5 = ((f32[64,1,2048]{2,1,0:T(1,128)}), f32[64,1,2048]{2,1,0:T(1,128)S(1)}, u32[]{:S(2)}, u32[]{:S(2)}) async-start(f32[64,1,2048]{2,1,0:T(1,128)} %broadcast_in_dim.31), calls=%async_computation.5 | async-start | bytes 1048576 | tf_op jit(solution)/shard_map/all_to_all | solution.py:155
  173.0 0.6 slice.185
  173.6 16.7 %all-to-all-done.5 = f32[64,1,2048]{2,1,0:T(1,128)S(1)} async-done(((f32[64,1,2048]{2,1,0:T(1,128)}), f32[64,1,2048]{2,1,0:T(1,128)S(1)}, u32[]{:S(2)}, u32[]{:S(2)}) %all-to-all-start.5) | async-done | bytes 524320 | tf_op jit(solution)/shard_map/all_to_all | solution.py:155
  190.3 1.2 reduce.2
  191.5 0.9 reshape.186
  (24 shorter events, 0.5 us)
Async XLA Ops:
  0.6 17.1 %copy-start.4 = (s32[1,1,64]{2,1,0:T(1,128)S(1)}, s32[1,1,64]{2,1,0:T(1,128)}, u32[]{:S(2)}) copy-start(s32[1,1,64]{2,1,0:T(1,128)} %param.13) | copy-start | bytes 772
  0.6 17.2 %copy-start.2 = (s32[1,1,64,32]{2,3,1,0:T(8,128)S(1)}, s32[1,1,64,32]{2,3,1,0:T(8,128)}, u32[]{:S(2)}) copy-start(s32[1,1,64,32]{2,3,1,0:T(8,128)} %param.12) | copy-start | bytes 24580
  4.7 28.9 %all-to-all-start = ((bf16[64,2,1792]{2,1,0:T(2,128)(2,1)}), bf16[64,2,1792]{2,1,0:T(2,128)(2,1)S(1)}, u32[]{:S(2)}, u32[]{:S(2)}) async-start(bf16[64,2,1792]{2,1,0:T(2,128)(2,1)} %pad_maximum_fusion.2), calls=%async_computation | async-start | bytes 917504 | tf_op jit(solution)/shard_map/all_to_all | solution.py:46
  36.3 9.3 %copy-start.3 = (s32[1,10,256]{2,0,1:T(1,128)S(1)}, s32[1,10,256]{2,0,1:T(1,128)}, u32[]{:S(2)}) copy-start(s32[1,10,256]{2,0,1:T(1,128)} %param.14) | copy-start | bytes 30724
  36.3 9.3 %copy-start.1 = (bf16[2,256,256]{2,1,0:T(8,128)(2,1)S(1)}, bf16[2,256,256]{2,1,0:T(8,128)(2,1)}, u32[]{:S(2)}) copy-start(bf16[2,256,256]{2,1,0:T(8,128)(2,1)} %param.11) | copy-start | bytes 786436
  39.3 34.8 %all-to-all-start.1 = ((bf16[64,32,256]{2,1,0:T(8,128)(2,1)}), bf16[64,32,256]{2,1,0:T(8,128)(2,1)S(1)}, u32[]{:S(2)}, u32[]{:S(2)}) async-start(bf16[64,32,256]{2,1,0:T(8,128)(2,1)} %bitcast.37), calls=%async_computation.1 | async-start | bytes 2097152 | tf_op jit(solution)/shard_map/all_to_all | solution.py:78
  74.1 3.2 %copy-start.5 = (bf16[1,256,256]{2,1,0:T(8,128)(2,1)S(1)}, bf16[1,256,256]{2,1,0:T(8,128)(2,1)}, u32[]{:S(2)}) copy-start(bf16[1,256,256]{2,1,0:T(8,128)(2,1)} %param.15) | copy-start | bytes 393220
  85.0 1.4 copy-start
  87.5 34.7 %all-to-all-start.2 = ((bf16[64,32,256]{2,1,0:T(8,128)(2,1)}), bf16[64,32,256]{2,1,0:T(8,128)(2,1)S(1)}, u32[]{:S(2)}, u32[]{:S(2)}) async-start(bf16[64,32,256]{2,1,0:T(8,128)(2,1)} %bitcast.43), calls=%async_computation.2 | async-start | bytes 2097152 | tf_op jit(solution)/shard_map/all_to_all | solution.py:121
  165.3 24.9 %all-to-all-start.5 = ((f32[64,1,2048]{2,1,0:T(1,128)}), f32[64,1,2048]{2,1,0:T(1,128)S(1)}, u32[]{:S(2)}, u32[]{:S(2)}) async-start(f32[64,1,2048]{2,1,0:T(1,128)} %broadcast_in_dim.31), calls=%async_computation.5 | async-start | bytes 1048576 | tf_op jit(solution)/shard_map/all_to_all | solution.py:155

commit v3 on v2

--- a/solution.py
+++ b/solution.py
@@ -14,6 +14,33 @@
 
 def elu_slope(pre):
     return jnp.where(pre > 0.0, jnp.ones_like(pre), jnp.exp(jnp.minimum(pre, 0.0)))
+
+
+def butterfly_reduce_scatter(pieces, steps):
+    for axis_name, bit in steps:
+        mine = (lax.axis_index(axis_name) >> bit) & 1
+        keep = lax.dynamic_index_in_dim(pieces, mine, axis=0, keepdims=False)
+        send = lax.dynamic_index_in_dim(pieces, 1 - mine, axis=0, keepdims=False)
+        size = lax.axis_size(axis_name)
+        pairs = [(i, i ^ (1 << bit)) for i in range(size)]
+        pieces = keep + lax.ppermute(send, axis_name, pairs)
+    return pieces
+
+
+def butterfly_all_gather(block, steps):
+    for axis_name, bit in reversed(steps):
+        mine = (lax.axis_index(axis_name) >> bit) & 1
+        size = lax.axis_size(axis_name)
+        pairs = [(i, i ^ (1 << bit)) for i in range(size)]
+        other = lax.ppermute(block, axis_name, pairs)
+        low = jnp.where(mine == 0, block, other)
+        high = jnp.where(mine == 0, other, block)
+        block = jnp.stack([low, high], axis=0)
+    return block
+
+
+def bit_steps(axis_name, size):
+    return [(axis_name, bit) for bit in range(size.bit_length() - 1)]
 
 
 def on_device(
@@ -107,6 +134,10 @@
             jnp.einsum("rh,rk->hk", aggregate_two, slope_two, preferred_element_type=jnp.float32),
         ]
     )
+    all_steps = bit_steps("feat", feat_devs) + bit_steps("rep", rep_devs)
+    two_shape = (2,) * len(all_steps) + (-1,)
+    two_block = butterfly_reduce_scatter(local_two.reshape(two_shape), all_steps)
+    grad_two = butterfly_all_gather(two_block, all_steps).reshape(local_two.shape)
     back_self = jnp.einsum(
         "rk,hk->rh", slope_two, weight_two[0], preferred_element_type=jnp.float32
     )
@@ -137,24 +168,15 @@
         ]
     )
 
-    one_part = jnp.transpose(
-        local_one.reshape(2, feat_devs, cols_dev, hidden_width), (1, 0, 2, 3)
-    ).reshape(feat_devs, -1)
-    two_part = local_two.reshape(feat_devs, -1)
-    outgoing_grad = jnp.concatenate([one_part, two_part], axis=1)
-    incoming_grad = lax.all_to_all(outgoing_grad, "feat", split_axis=0, concat_axis=0, tiled=True)
-    feat_summed = jnp.sum(incoming_grad, axis=0)
-    rep_copies = jnp.broadcast_to(feat_summed[None], (rep_devs,) + feat_summed.shape)
-    reduced = jnp.sum(
-        lax.all_to_all(rep_copies, "rep", split_axis=0, concat_axis=0, tiled=True), axis=0
-    )
-    one_size = one_part.shape[1]
-    grad_one = reduced[:one_size].reshape(2, cols_dev, hidden_width)
-    two_piece = reduced[one_size:]
-    two_copies = jnp.broadcast_to(two_piece[None], (feat_devs,) + two_piece.shape)
-    grad_two = lax.all_to_all(
-        two_copies, "feat", split_axis=0, concat_axis=0, tiled=True
-    ).reshape(local_two.shape)
+    feat_steps = bit_steps("feat", feat_devs)
+    bits = len(feat_steps)
+    one_split = local_one.reshape((2,) + (2,) * bits + (cols_dev, hidden_width))
+    order = tuple(range(bits, 0, -1)) + (0, bits + 1, bits + 2)
+    one_block = butterfly_reduce_scatter(jnp.transpose(one_split, order), feat_steps)
+    for axis_name, bit in bit_steps("rep", rep_devs):
+        pairs = [(i, i ^ (1 << bit)) for i in range(rep_devs)]
+        one_block = one_block + lax.ppermute(one_block, axis_name, pairs)
+    grad_one = one_block
     return (hidden_two[None], grad_one, grad_two)
 
 

time: 193 us -> 197 us (1.021)
  the two profiles are of different devices: /device:TPU:1 before, /device:TPU:22 now
where the time goes in v3:
time: 197 us; the launch traced here: 196 us
  waiting for transfers between devices  107 us (54%)
  starting transfers between devices  56.2 us (29%)
  matrix products  19.9 us (10%)
  local copies, waits for them, and re-layouts  7.26 us (4%)
  other arithmetic  4.66 us (2%)
    ppermute x14, waiting for transfers between devices, butterfly_reduce_scatter(): pieces = keep + lax.ppermute(send, axis_name, pairs)  42.9 us
    all_to_all x1, waiting for transfers between devices, on_device(): lax.all_to_all(outgoing.reshape(peers, capacity, hidden_width), 'feat', s...  26.4 us
    ppermute x8, waiting for transfers between devices, butterfly_all_gather(): other = lax.ppermute(block, axis_name, pairs)  17.8 us
    ppermute x14, starting transfers between devices, butterfly_reduce_scatter(): pieces = keep + lax.ppermute(send, axis_name, pairs)  15.6 us
    all_to_all x1, waiting for transfers between devices, on_device(): lax.all_to_all(outgoing_one, 'feat', split_axis=0, concat_axis=0, tiled=T...  14.3 us
    ppermute x8, starting transfers between devices, butterfly_all_gather(): other = lax.ppermute(block, axis_name, pairs)  12.8 us
    all_to_all x1, starting transfers between devices, on_device(): lax.all_to_all(outgoing_one, 'feat', split_axis=0, concat_axis=0, tiled=T...  12.2 us
    all_to_all x1, starting transfers between devices, on_device(): lax.all_to_all(grad_table[node_count:].reshape(peers, capacity, hidden_wi...  7.12 us
  transfers between devices with their start and end apart: 27, of which 21 were waited for; matrix products, arithmetic and copies ran while one was open for 7% of the time, Pallas kernels for 0%

profile of v3, /device:TPU:22, one launch (start us, length us, event | category | flops | bytes accessed | tf_op | source)
XLA Modules:
  0.0 196.2 jit_solution(2690893339036576744)
XLA Ops:
  1.6 0.9 copy.62
  3.5 1.2 pad_maximum_fusion.1
  4.7 12.2 %all-to-all-start = ((bf16[64,2,1792]{2,1,0:T(2,128)(2,1)}), bf16[64,2,1792]{2,1,0:T(2,128)(2,1)S(1)}, u32[]{:S(2)}, u32[]{:S(2)}) async-start(bf16[64,2,1792]{2,1,0:T(2,128)(2,1)} %pad_maximum_fusion.1), calls=%async_computation | async-start | bytes 917504 | tf_op jit(solution)/shard_map/all_to_all | solution.py:73
  18.0 14.3 %all-to-all-done = bf16[64,2,1792]{2,1,0:T(2,128)(2,1)S(1)} async-done(((bf16[64,2,1792]{2,1,0:T(2,128)(2,1)}), bf16[64,2,1792]{2,1,0:T(2,128)(2,1)S(1)}, u32[]{:S(2)}, u32[]{:S(2)}) %all-to-all-start) | async-done | bytes 458784 | tf_op jit(solution)/shard_map/all_to_all | solution.py:73
  32.8 2.2 %fusion.27 = bf16[128,256]{1,0:T(8,128)(2,1)S(1)} fusion(s32[256]{0:T(256)S(1)} %bitcast.221, s32[256]{0:T(256)S(1)} %bitcast.222, s32[256]{0:T(256)S(1)} %bitcast.223, s32[256]{0:T(256)S(1)} %bitcast.224, s32[256]{0:T(256)S(1)} %bitcast.225, s32[256]{0:T(256)S(1)} %bitcast.226, s32[256]{0:T(256)S(1)} %bitcast.227, s32[256]{0:T(256)S(1)} %bitcast.228, ...), kind=kOutput, calls=%fused_computation.35 | convolution fusion | flops 78970880 | bytes 343040 | tf_op jit(solution)/shard_map/fs,vs->fv/dot_general | solution.py:87
  35.3 2.6 %convolution_convert_fusion = bf16[2048,256]{1,0:T(8,128)(2,1)} fusion(bf16[256,256]{1,0:T(8,128)(2,1)S(1)} %get-tuple-element.50, s32[2048]{0:T(1024)S(1)} %eq.374, pred[2048]{0:T(1024)(128)(4,1)S(1)} %lt.99), kind=kOutput, calls=%fused_computation | convolution fusion | flops 270008320 | bytes 1189888 | tf_op jit(solution)/shard_map/ji,ih->jh/dot_general | solution.py:102
  38.0 6.8 %all-to-all-start.1 = ((bf16[64,32,256]{2,1,0:T(8,128)(2,1)}), bf16[64,32,256]{2,1,0:T(8,128)(2,1)S(1)}, u32[]{:S(2)}, u32[]{:S(2)}) async-start(bf16[64,32,256]{2,1,0:T(8,128)(2,1)} %bitcast.37), calls=%async_computation.1 | async-start | bytes 2097152 | tf_op jit(solution)/shard_map/all_to_all | solution.py:105
  45.0 26.4 %all-to-all-done.1 = bf16[64,32,256]{2,1,0:T(8,128)(2,1)S(1)} async-done(((bf16[64,32,256]{2,1,0:T(8,128)(2,1)}), bf16[64,32,256]{2,1,0:T(8,128)(2,1)S(1)}, u32[]{:S(2)}, u32[]{:S(2)}) %all-to-all-start.1) | async-done | bytes 1048608 | tf_op jit(solution)/shard_map/all_to_all | solution.py:105
  71.4 3.2 %fusion.21 = bf16[256,256]{1,0:T(8,128)(2,1)S(1)} fusion(bf16[2048,256]{1,0:T(8,128)(2,1)S(1)} %bitcast.184, bf16[256,256]{1,0:T(8,128)(2,1)S(1)} %get-tuple-element.50, s32[256]{0:T(256)S(1)} %bitcast.216, s32[256]{0:T(256)S(1)} %bitcast.218, s32[256]{0:T(256)S(1)} %bitcast.202, s32[256]{0:T(256)S(1)} %bitcast.204, s32[256]{0:T(256)S(1)} %bitcast.206, ...), kind=kOutput, calls=%fused_computation.32 | convolution fusion | flops 322174976 | bytes 1320960 | tf_op jit(solution)/shard_map/dr,rh->dh/dot_general | solution.py:119
  74.6 1.0 fusion.52
  76.5 2.0 %collective-permute-start.8 = (f32[2,2,2,2,2,2,2,512]{7,6,5,4,3,2,1,0:T(2,128)S(1)}, f32[2,2,2,2,2,2,2,512]{7,6,5,4,3,2,1,0:T(2,128)S(1)}, u32[]{:S(2)}, u32[]{:S(2)}) collective-permute-start(f32[2,2,2,2,2,2,2,512]{7,6,5,4,3,2,1,0:T(2,128)S(1)} %dynamic-slice_bitcast_fusion), channel_id=1, source_target_pairs={{0,4},{4,0},{8,12},{12,8},{16,20},{20,16},{24,28},{28,24},{32,36},... | collective-permute-start | bytes 786440 | tf_op jit(solution)/shard_map/ppermute | solution.py:26
  78.4 1.2 collective-permute-done.8
  80.4 5.2 %collective-permute-done.9 = f32[2,2,2,2,2,2,512]{6,5,4,3,2,1,0:T(2,128)S(1)} collective-permute-done((f32[2,2,2,2,2,2,512]{6,5,4,3,2,1,0:T(2,128)S(1)}, f32[2,2,2,2,2,2,512]{6,5,4,3,2,1,0:T(2,128)S(1)}, u32[]{:S(2)}, u32[]{:S(2)}) %collective-permute-start.9) | collective-permute-done | bytes 131104 | tf_op jit(solution)/shard_map/ppermute | solution.py:26
  86.3 5.6 %collective-permute-done.10 = f32[2,2,2,2,2,512]{5,4,3,2,1,0:T(2,128)S(1)} collective-permute-done((f32[2,2,2,2,2,512]{5,4,3,2,1,0:T(2,128)S(1)}, f32[2,2,2,2,2,512]{5,4,3,2,1,0:T(2,128)S(1)}, u32[]{:S(2)}, u32[]{:S(2)}) %collective-permute-start.10) | collective-permute-done | bytes 65568 | tf_op jit(solution)/shard_map/ppermute | solution.py:26
  91.9 0.9 collective-permute-start.11
  92.9 7.0 %collective-permute-done.11 = f32[2,2,2,2,512]{4,3,2,1,0:T(2,128)S(1)} collective-permute-done((f32[2,2,2,2,512]{4,3,2,1,0:T(2,128)S(1)}, f32[2,2,2,2,512]{4,3,2,1,0:T(2,128)S(1)}, u32[]{:S(2)}, u32[]{:S(2)}) %collective-permute-start.11) | collective-permute-done | bytes 32800 | tf_op jit(solution)/shard_map/ppermute | solution.py:26
  99.9 1.1 collective-permute-start.12
  101.3 2.4 %collective-permute-done.12 = f32[2,2,2,512]{3,2,1,0:T(2,128)S(1)} collective-permute-done((f32[2,2,2,512]{3,2,1,0:T(2,128)S(1)}, f32[2,2,2,512]{3,2,1,0:T(2,128)S(1)}, u32[]{:S(2)}, u32[]{:S(2)}) %collective-permute-start.12) | collective-permute-done | bytes 16416 | tf_op jit(solution)/shard_map/ppermute | solution.py:26
  103.7 1.3 collective-permute-start.13
  105.1 6.5 %fusion.10 = f32[2304,256]{1,0:T(8,128)S(1)} fusion(f32[256,256]{1,0:T(8,128)S(1)} %convolution_multiply_fusion, s32[256]{0:T(256)S(1)} %bitcast.217, s32[256]{0:T(256)S(1)} %bitcast.219, s32[256]{0:T(256)S(1)} %bitcast.203, s32[256]{0:T(256)S(1)} %bitcast.205, s32[256]{0:T(256)S(1)} %bitcast.207, s32[256]{0:T(256)S(1)} %bitcast.209, s32[256]{0:T(256)S(1)} %bitcast.211, ...), kind=kOutput, calls=%fused_computation.23 | convolution fusion | flops 1829044224 | bytes 2631680 | tf_op jit(solution)/shard_map/dr,dh->rh/dot_general | solution.py:148
  111.6 1.4 copy-done
  113.1 1.1 slice.219
  114.1 7.1 %all-to-all-start.2 = ((bf16[64,32,256]{2,1,0:T(8,128)(2,1)}), bf16[64,32,256]{2,1,0:T(8,128)(2,1)S(1)}, u32[]{:S(2)}, u32[]{:S(2)}) async-start(bf16[64,32,256]{2,1,0:T(8,128)(2,1)} %bitcast.43), calls=%async_computation.2 | async-start | bytes 2097152 | tf_op jit(solution)/shard_map/all_to_all | solution.py:152
  121.3 1.4 collective-permute-start.14
  122.7 2.3 %collective-permute-done.14 = f32[2,512]{1,0:T(2,128)S(1)} collective-permute-done((f32[2,512]{1,0:T(2,128)S(1)}, f32[2,512]{1,0:T(2,128)S(1)}, u32[]{:S(2)}, u32[]{:S(2)}) %collective-permute-start.14) | collective-permute-done | bytes 4128 | tf_op jit(solution)/shard_map/ppermute | solution.py:26
  125.5 4.8 %collective-permute-done.15 = f32[512]{0:T(512)S(1)} collective-permute-done((f32[512]{0:T(512)S(1)}, f32[512]{0:T(512)S(1)}, u32[]{:S(2)}, u32[]{:S(2)}) %collective-permute-start.15) | collective-permute-done | bytes 2080 | tf_op jit(solution)/shard_map/ppermute | solution.py:26
  130.5 4.8 %collective-permute-done.16 = f32[512]{0:T(512)S(1)} collective-permute-done((f32[512]{0:T(512)S(1)}, f32[512]{0:T(512)S(1)}, u32[]{:S(2)}, u32[]{:S(2)}) %collective-permute-start.16) | collective-permute-done | bytes 2080 | tf_op jit(solution)/shard_map/ppermute | solution.py:35
  135.3 1.6 collective-permute-start.17
  136.9 2.3 %collective-permute-done.17 = f32[2,512]{1,0:T(2,128)S(1)} collective-permute-done((f32[2,512]{1,0:T(2,128)S(1)}, f32[2,512]{1,0:T(2,128)S(1)}, u32[]{:S(2)}, u32[]{:S(2)}) %collective-permute-start.17) | collective-permute-done | bytes 4128 | tf_op jit(solution)/shard_map/ppermute | solution.py:35
  139.3 1.3 collective-permute-start.18
  140.6 4.0 %collective-permute-done.18 = f32[2,2,512]{2,1,0:T(2,128)S(1)} collective-permute-done((f32[2,2,512]{2,1,0:T(2,128)S(1)}, f32[2,2,512]{2,1,0:T(2,128)S(1)}, u32[]{:S(2)}, u32[]{:S(2)}) %collective-permute-start.18) | collective-permute-done | bytes 8224 | tf_op jit(solution)/shard_map/ppermute | solution.py:35
  145.6 2.9 %collective-permute-done.19 = f32[2,2,2,512]{3,2,1,0:T(2,128)S(1)} collective-permute-done((f32[2,2,2,512]{3,2,1,0:T(2,128)S(1)}, f32[2,2,2,512]{3,2,1,0:T(2,128)S(1)}, u32[]{:S(2)}, u32[]{:S(2)}) %collective-permute-start.19) | collective-permute-done | bytes 16416 | tf_op jit(solution)/shard_map/ppermute | solution.py:35
  148.5 5.5 %collective-permute-start.20 = (f32[2,2,2,2,512]{4,3,2,1,0:T(2,128)S(1)}, f32[2,2,2,2,512]{4,3,2,1,0:T(2,128)S(1)}, u32[]{:S(2)}, u32[]{:S(2)}) collective-permute-start(f32[2,2,2,2,512]{4,3,2,1,0:T(2,128)S(1)} %pad_maximum_fusion.5), channel_id=1, source_target_pairs={{0,32},{4,36},{8,40},{12,44},{16,48},{20,52},{24,56},{28,60},{32,0... | collective-permute-start | bytes 98312 | tf_op jit(solution)/shard_map/ppermute | solution.py:35
  154.0 1.5 fusion.13
  155.6 1.2 fusion.26
  157.5 1.7 collective-permute-start.21
  159.4 1.2 collective-permute-start.1
  160.6 3.9 %collective-permute-done.21 = f32[2,2,2,2,2,512]{5,4,3,2,1,0:T(2,128)S(1)} collective-permute-done((f32[2,2,2,2,2,512]{5,4,3,2,1,0:T(2,128)S(1)}, f32[2,2,2,2,2,512]{5,4,3,2,1,0:T(2,128)S(1)}, u32[]{:S(2)}, u32[]{:S(2)}) %collective-permute-start.21) | collective-permute-done | bytes 65568 | tf_op jit(solution)/shard_map/ppermute | solution.py:35
  165.3 1.4 collective-permute-start.22
  166.6 3.4 %collective-permute-done.2 = f32[2,2,2,2,2,256]{5,4,3,2,1,0:T(2,128)S(1)} collective-permute-done((f32[2,2,2,2,2,256]{5,4,3,2,1,0:T(2,128)S(1)}, f32[2,2,2,2,2,256]{5,4,3,2,1,0:T(2,128)S(1)}, u32[]{:S(2)}, u32[]{:S(2)}) %collective-permute-start.2) | collective-permute-done | bytes 32800 | tf_op jit(solution)/shard_map/ppermute | solution.py:26
  170.1 3.6 %collective-permute-start.3 = (f32[2,2,2,2,256]{4,3,2,1,0:T(2,128)S(1)}, f32[2,2,2,2,256]{4,3,2,1,0:T(2,128)S(1)}, u32[]{:S(2)}, u32[]{:S(2)}) collective-permute-start(f32[2,2,2,2,256]{4,3,2,1,0:T(2,128)S(1)} %dynamic-slice_bitcast_fusion.7), channel_id=1, source_target_pairs={{0,32},{4,36},{8,40},{12,44},{16,48},{20,52},{24,56},{28,60},{32,0... | collective-permute-start | bytes 49160 | tf_op jit(solution)/shard_map/ppermute | solution.py:26
  173.8 4.0 %collective-permute-done.3 = f32[2,2,2,2,256]{4,3,2,1,0:T(2,128)S(1)} collective-permute-done((f32[2,2,2,2,256]{4,3,2,1,0:T(2,128)S(1)}, f32[2,2,2,2,256]{4,3,2,1,0:T(2,128)S(1)}, u32[]{:S(2)}, u32[]{:S(2)}) %collective-permute-start.3) | collective-permute-done | bytes 16416 | tf_op jit(solution)/shard_map/ppermute | solution.py:26
  179.0 2.7 %collective-permute-done.4 = f32[2,2,2,256]{3,2,1,0:T(2,128)S(1)} collective-permute-done((f32[2,2,2,256]{3,2,1,0:T(2,128)S(1)}, f32[2,2,2,256]{3,2,1,0:T(2,128)S(1)}, u32[]{:S(2)}, u32[]{:S(2)}) %collective-permute-start.4) | collective-permute-done | bytes 8224 | tf_op jit(solution)/shard_map/ppermute | solution.py:26
  181.6 1.4 collective-permute-start.5
  183.1 3.8 %collective-permute-done.5 = f32[2,2,256]{2,1,0:T(2,128)S(1)} collective-permute-done((f32[2,2,256]{2,1,0:T(2,128)S(1)}, f32[2,2,256]{2,1,0:T(2,128)S(1)}, u32[]{:S(2)}, u32[]{:S(2)}) %collective-permute-start.5) | collective-permute-done | bytes 4128 | tf_op jit(solution)/shard_map/ppermute | solution.py:26
  186.9 1.3 collective-permute-start.6
  188.9 1.6 collective-permute-done.6
  191.6 4.0 %collective-permute-done.7 = f32[2,2,256]{2,1,0:T(2,128)S(1)} collective-permute-done((f32[2,2,256]{2,1,0:T(2,128)S(1)}, f32[2,2,256]{2,1,0:T(2,128)S(1)}, u32[]{:S(2)}, u32[]{:S(2)}) %collective-permute-start.7) | collective-permute-done | bytes 4128 | tf_op jit(solution)/shard_map/ppermute | solution.py:178
  (108 shorter events, 13.7 us)
Async XLA Ops:
  0.6 16.3 %copy-start.2 = (s32[1,1,64,32]{2,3,1,0:T(8,128)S(1)}, s32[1,1,64,32]{2,3,1,0:T(8,128)}, u32[]{:S(2)}) copy-start(s32[1,1,64,32]{2,3,1,0:T(8,128)} %param.12) | copy-start | bytes 24580
  0.6 16.4 %copy-start.4 = (s32[1,1,64]{2,1,0:T(1,128)S(1)}, s32[1,1,64]{2,1,0:T(1,128)}, u32[]{:S(2)}) copy-start(s32[1,1,64]{2,1,0:T(1,128)} %param.13) | copy-start | bytes 772
  4.7 27.6 %all-to-all-start = ((bf16[64,2,1792]{2,1,0:T(2,128)(2,1)}), bf16[64,2,1792]{2,1,0:T(2,128)(2,1)S(1)}, u32[]{:S(2)}, u32[]{:S(2)}) async-start(bf16[64,2,1792]{2,1,0:T(2,128)(2,1)} %pad_maximum_fusion.1), calls=%async_computation | async-start | bytes 917504 | tf_op jit(solution)/shard_map/all_to_all | solution.py:73
  35.0 9.8 %copy-start.3 = (s32[1,10,256]{2,0,1:T(1,128)S(1)}, s32[1,10,256]{2,0,1:T(1,128)}, u32[]{:S(2)}) copy-start(s32[1,10,256]{2,0,1:T(1,128)} %param.14) | copy-start | bytes 30724
  35.0 9.8 %copy-start.1 = (bf16[2,256,256]{2,1,0:T(8,128)(2,1)S(1)}, bf16[2,256,256]{2,1,0:T(8,128)(2,1)}, u32[]{:S(2)}) copy-start(bf16[2,256,256]{2,1,0:T(8,128)(2,1)} %param.11) | copy-start | bytes 786436
  38.0 33.4 %all-to-all-start.1 = ((bf16[64,32,256]{2,1,0:T(8,128)(2,1)}), bf16[64,32,256]{2,1,0:T(8,128)(2,1)S(1)}, u32[]{:S(2)}, u32[]{:S(2)}) async-start(bf16[64,32,256]{2,1,0:T(8,128)(2,1)} %bitcast.37), calls=%async_computation.1 | async-start | bytes 2097152 | tf_op jit(solution)/shard_map/all_to_all | solution.py:105
  71.4 3.2 %copy-start.5 = (bf16[1,256,256]{2,1,0:T(8,128)(2,1)S(1)}, bf16[1,256,256]{2,1,0:T(8,128)(2,1)}, u32[]{:S(2)}) copy-start(bf16[1,256,256]{2,1,0:T(8,128)(2,1)} %param.15) | copy-start | bytes 393220
  76.5 3.2 %collective-permute-start.8 = (f32[2,2,2,2,2,2,2,512]{7,6,5,4,3,2,1,0:T(2,128)S(1)}, f32[2,2,2,2,2,2,2,512]{7,6,5,4,3,2,1,0:T(2,128)S(1)}, u32[]{:S(2)}, u32[]{:S(2)}) collective-permute-start(f32[2,2,2,2,2,2,2,512]{7,6,5,4,3,2,1,0:T(2,128)S(1)} %dynamic-slice_bitcast_fusion), channel_id=1, source_target_pairs={{0,4},{4,0},{8,12},{12,8},{16,20},{20,16},{24,28},{28,24},{32,36},... | collective-permute-start | bytes 786440 | tf_op jit(solution)/shard_map/ppermute | solution.py:26
  79.8 5.9 %collective-permute-start.9 = (f32[2,2,2,2,2,2,512]{6,5,4,3,2,1,0:T(2,128)S(1)}, f32[2,2,2,2,2,2,512]{6,5,4,3,2,1,0:T(2,128)S(1)}, u32[]{:S(2)}, u32[]{:S(2)}) collective-permute-start(f32[2,2,2,2,2,2,512]{6,5,4,3,2,1,0:T(2,128)S(1)} %dynamic-slice_bitcast_fusion.1), channel_id=1, source_target_pairs={{0,8},{4,12},{8,0},{12,4},{16,24},{20,28},{24,16},{28,20},{32,40},... | collective-permute-start | bytes 393224 | tf_op jit(solution)/shard_map/ppermute | solution.py:26
  85.7 6.1 %collective-permute-start.10 = (f32[2,2,2,2,2,512]{5,4,3,2,1,0:T(2,128)S(1)}, f32[2,2,2,2,2,512]{5,4,3,2,1,0:T(2,128)S(1)}, u32[]{:S(2)}, u32[]{:S(2)}) collective-permute-start(f32[2,2,2,2,2,512]{5,4,3,2,1,0:T(2,128)S(1)} %dynamic-slice_bitcast_fusion.3), channel_id=1, source_target_pairs={{0,16},{4,20},{8,24},{12,28},{16,0},{20,4},{24,8},{28,12},{32,48},... | collective-permute-start | bytes 196616 | tf_op jit(solution)/shard_map/ppermute | solution.py:26
  91.9 7.9 %collective-permute-start.11 = (f32[2,2,2,2,512]{4,3,2,1,0:T(2,128)S(1)}, f32[2,2,2,2,512]{4,3,2,1,0:T(2,128)S(1)}, u32[]{:S(2)}, u32[]{:S(2)}) collective-permute-start(f32[2,2,2,2,512]{4,3,2,1,0:T(2,128)S(1)} %dynamic-slice_bitcast_fusion.4), channel_id=1, source_target_pairs={{0,32},{4,36},{8,40},{12,44},{16,48},{20,52},{24,56},{28,60},{32,0... | collective-permute-start | bytes 98312 | tf_op jit(solution)/shard_map/ppermute | solution.py:26
  99.9 3.8 %collective-permute-start.12 = (f32[2,2,2,512]{3,2,1,0:T(2,128)S(1)}, f32[2,2,2,512]{3,2,1,0:T(2,128)S(1)}, u32[]{:S(2)}, u32[]{:S(2)}) collective-permute-start(f32[2,2,2,512]{3,2,1,0:T(2,128)S(1)} %dynamic-slice_bitcast_fusion.6), channel_id=1, source_target_pairs={{0,64},{4,68},{8,72},{12,76},{16,80},{20,84},{24,88},{28,92},{32,9... | collective-permute-start | bytes 49160 | tf_op jit(solution)/shard_map/ppermute | solution.py:26
  103.7 17.5 %collective-permute-start.13 = (f32[2,2,512]{2,1,0:T(2,128)S(1)}, f32[2,2,512]{2,1,0:T(2,128)S(1)}, u32[]{:S(2)}, u32[]{:S(2)}) collective-permute-start(f32[2,2,512]{2,1,0:T(2,128)S(1)} %dynamic-slice_bitcast_fusion.8), channel_id=1, source_target_pairs={{0,128},{4,132},{8,136},{12,140},{16,144},{20,148},{24,152},{28,15... | collective-permute-start | bytes 24584 | tf_op jit(solution)/shard_map/ppermute | solution.py:26
  111.6 1.4 copy-start
  114.1 39.9 %all-to-all-start.2 = ((bf16[64,32,256]{2,1,0:T(8,128)(2,1)}), bf16[64,32,256]{2,1,0:T(8,128)(2,1)S(1)}, u32[]{:S(2)}, u32[]{:S(2)}) async-start(bf16[64,32,256]{2,1,0:T(8,128)(2,1)} %bitcast.43), calls=%async_computation.2 | async-start | bytes 2097152 | tf_op jit(solution)/shard_map/all_to_all | solution.py:152
  121.3 3.7 %collective-permute-start.14 = (f32[2,512]{1,0:T(2,128)S(1)}, f32[2,512]{1,0:T(2,128)S(1)}, u32[]{:S(2)}, u32[]{:S(2)}) collective-permute-start(f32[2,512]{1,0:T(2,128)S(1)} %fusion.73), channel_id=1, source_target_pairs={{0,1},{1,0},{2,3},{3,2},{4,5},{5,4},{6,7},{7,6},{8,9},{9,8},{10,11... | collective-permute-start | bytes 12296 | tf_op jit(solution)/shard_map/ppermute | solution.py:26
  125.0 5.2 %collective-permute-start.15 = (f32[512]{0:T(512)S(1)}, f32[512]{0:T(512)S(1)}, u32[]{:S(2)}, u32[]{:S(2)}) collective-permute-start(f32[512]{0:T(512)S(1)} %bitcast.199), channel_id=1, source_target_pairs={{0,2},{1,3},{2,0},{3,1},{4,6},{5,7},{6,4},{7,5},{8,10},{9,11},{10,... | collective-permute-start | bytes 6152 | tf_op jit(solution)/shard_map/ppermute | solution.py:26
  130.2 5.1 %collective-permute-start.16 = (f32[512]{0:T(512)S(1)}, f32[512]{0:T(512)S(1)}, u32[]{:S(2)}, u32[]{:S(2)}) collective-permute-start(f32[512]{0:T(512)S(1)} %add.274), channel_id=1, source_target_pairs={{0,2},{1,3},{2,0},{3,1},{4,6},{5,7},{6,4},{7,5},{8,10},{9,11},{10,... | collective-permute-start | bytes 6152 | tf_op jit(solution)/shard_map/ppermute | solution.py:35
  135.3 3.9 %collective-permute-start.17 = (f32[2,512]{1,0:T(2,128)S(1)}, f32[2,512]{1,0:T(2,128)S(1)}, u32[]{:S(2)}, u32[]{:S(2)}) collective-permute-start(f32[2,512]{1,0:T(2,128)S(1)} %pad_maximum_fusion.8), channel_id=1, source_target_pairs={{0,1},{1,0},{2,3},{3,2},{4,5},{5,4},{6,7},{7,6},{8,9},{9,8},{10,11... | collective-permute-start | bytes 12296 | tf_op jit(solution)/shard_map/ppermute | solution.py:35
  139.3 5.3 %collective-permute-start.18 = (f32[2,2,512]{2,1,0:T(2,128)S(1)}, f32[2,2,512]{2,1,0:T(2,128)S(1)}, u32[]{:S(2)}, u32[]{:S(2)}) collective-permute-start(f32[2,2,512]{2,1,0:T(2,128)S(1)} %pad_maximum_fusion.7), channel_id=1, source_target_pairs={{0,128},{4,132},{8,136},{12,140},{16,144},{20,148},{24,152},{28,15... | collective-permute-start | bytes 24584 | tf_op jit(solution)/shard_map/ppermute | solution.py:35
  144.6 3.8 %collective-permute-start.19 = (f32[2,2,2,512]{3,2,1,0:T(2,128)S(1)}, f32[2,2,2,512]{3,2,1,0:T(2,128)S(1)}, u32[]{:S(2)}, u32[]{:S(2)}) collective-permute-start(f32[2,2,2,512]{3,2,1,0:T(2,128)S(1)} %pad_maximum_fusion.6), channel_id=1, source_target_pairs={{0,64},{4,68},{8,72},{12,76},{16,80},{20,84},{24,88},{28,92},{32,9... | collective-permute-start | bytes 49160 | tf_op jit(solution)/shard_map/ppermute | solution.py:35
  148.5 8.9 %collective-permute-start.20 = (f32[2,2,2,2,512]{4,3,2,1,0:T(2,128)S(1)}, f32[2,2,2,2,512]{4,3,2,1,0:T(2,128)S(1)}, u32[]{:S(2)}, u32[]{:S(2)}) collective-permute-start(f32[2,2,2,2,512]{4,3,2,1,0:T(2,128)S(1)} %pad_maximum_fusion.5), channel_id=1, source_target_pairs={{0,32},{4,36},{8,40},{12,44},{16,48},{20,52},{24,56},{28,60},{32,0... | collective-permute-start | bytes 98312 | tf_op jit(solution)/shard_map/ppermute | solution.py:35
  157.3 1.9 collective-permute-start
  157.5 7.0 %collective-permute-start.21 = (f32[2,2,2,2,2,512]{5,4,3,2,1,0:T(2,128)S(1)}, f32[2,2,2,2,2,512]{5,4,3,2,1,0:T(2,128)S(1)}, u32[]{:S(2)}, u32[]{:S(2)}) collective-permute-start(f32[2,2,2,2,2,512]{5,4,3,2,1,0:T(2,128)S(1)} %pad_maximum_fusion.4), channel_id=1, source_target_pairs={{0,16},{4,20},{8,24},{12,28},{16,0},{20,4},{24,8},{28,12},{32,48},... | collective-permute-start | bytes 196616 | tf_op jit(solution)/shard_map/ppermute | solution.py:35
  159.4 5.6 %collective-permute-start.1 = (f32[2,2,2,2,2,2,256]{6,5,4,3,2,1,0:T(2,128)S(1)}, f32[2,2,2,2,2,2,256]{6,5,4,3,2,1,0:T(2,128)S(1)}, u32[]{:S(2)}, u32[]{:S(2)}) collective-permute-start(f32[2,2,2,2,2,2,256]{6,5,4,3,2,1,0:T(2,128)S(1)} %bitcast.191), channel_id=1, source_target_pairs={{0,8},{4,12},{8,0},{12,4},{16,24},{20,28},{24,16},{28,20},{32,40},... | collective-permute-start | bytes 196616 | tf_op jit(solution)/shard_map/ppermute | solution.py:26
  165.1 5.0 %collective-permute-start.2 = (f32[2,2,2,2,2,256]{5,4,3,2,1,0:T(2,128)S(1)}, f32[2,2,2,2,2,256]{5,4,3,2,1,0:T(2,128)S(1)}, u32[]{:S(2)}, u32[]{:S(2)}) collective-permute-start(f32[2,2,2,2,2,256]{5,4,3,2,1,0:T(2,128)S(1)} %dynamic-slice_bitcast_fusion.5), channel_id=1, source_target_pairs={{0,16},{4,20},{8,24},{12,28},{16,0},{20,4},{24,8},{28,12},{32,48},... | collective-permute-start | bytes 98312 | tf_op jit(solution)/shard_map/ppermute | solution.py:26
  165.3 8.4 %collective-permute-start.22 = (f32[2,2,2,2,2,2,512]{6,5,4,3,2,1,0:T(2,128)S(1)}, f32[2,2,2,2,2,2,512]{6,5,4,3,2,1,0:T(2,128)S(1)}, u32[]{:S(2)}, u32[]{:S(2)}) collective-permute-start(f32[2,2,2,2,2,2,512]{6,5,4,3,2,1,0:T(2,128)S(1)} %pad_maximum_fusion.3), channel_id=1, source_target_pairs={{0,8},{4,12},{8,0},{12,4},{16,24},{20,28},{24,16},{28,20},{32,40},... | collective-permute-start | bytes 393224 | tf_op jit(solution)/shard_map/ppermute | solution.py:35
  170.1 7.7 %collective-permute-start.3 = (f32[2,2,2,2,256]{4,3,2,1,0:T(2,128)S(1)}, f32[2,2,2,2,256]{4,3,2,1,0:T(2,128)S(1)}, u32[]{:S(2)}, u32[]{:S(2)}) collective-permute-start(f32[2,2,2,2,256]{4,3,2,1,0:T(2,128)S(1)} %dynamic-slice_bitcast_fusion.7), channel_id=1, source_target_pairs={{0,32},{4,36},{8,40},{12,44},{16,48},{20,52},{24,56},{28,60},{32,0... | collective-permute-start | bytes 49160 | tf_op jit(solution)/shard_map/ppermute | solution.py:26
  177.9 3.7 %collective-permute-start.4 = (f32[2,2,2,256]{3,2,1,0:T(2,128)S(1)}, f32[2,2,2,256]{3,2,1,0:T(2,128)S(1)}, u32[]{:S(2)}, u32[]{:S(2)}) collective-permute-start(f32[2,2,2,256]{3,2,1,0:T(2,128)S(1)} %dynamic-slice_bitcast_fusion.9), channel_id=1, source_target_pairs={{0,64},{4,68},{8,72},{12,76},{16,80},{20,84},{24,88},{28,92},{32,9... | collective-permute-start | bytes 24584 | tf_op jit(solution)/shard_map/ppermute | solution.py:26
  178.9 9.3 %collective-permute-start.23 = (f32[2,2,2,2,2,2,2,512]{7,6,5,4,3,2,1,0:T(2,128)S(1)}, f32[2,2,2,2,2,2,2,512]{7,6,5,4,3,2,1,0:T(2,128)S(1)}, u32[]{:S(2)}, u32[]{:S(2)}) collective-permute-start(f32[2,2,2,2,2,2,2,512]{7,6,5,4,3,2,1,0:T(2,128)S(1)} %pad_maximum_fusion.2), channel_id=1, source_target_pairs={{0,4},{4,0},{8,12},{12,8},{16,20},{20,16},{24,28},{28,24},{32,36},... | collective-permute-start | bytes 786440 | tf_op jit(solution)/shard_map/ppermute | solution.py:35
  181.6 5.2 %collective-permute-start.5 = (f32[2,2,256]{2,1,0:T(2,128)S(1)}, f32[2,2,256]{2,1,0:T(2,128)S(1)}, u32[]{:S(2)}, u32[]{:S(2)}) collective-permute-start(f32[2,2,256]{2,1,0:T(2,128)S(1)} %fusion.70), channel_id=1, source_target_pairs={{0,128},{4,132},{8,136},{12,140},{16,144},{20,148},{24,152},{28,15... | collective-permute-start | bytes 12296 | tf_op jit(solution)/shard_map/ppermute | solution.py:26
  186.9 3.6 %collective-permute-start.6 = (f32[2,2,256]{2,1,0:T(2,128)S(1)}, f32[2,2,256]{2,1,0:T(2,128)S(1)}, u32[]{:S(2)}, u32[]{:S(2)}) collective-permute-start(f32[2,2,256]{2,1,0:T(2,128)S(1)} %fusion.69), channel_id=1, source_target_pairs={{0,1},{1,0},{2,3},{3,2},{4,5},{5,4},{6,7},{7,6},{8,9},{9,8},{10,11... | collective-permute-start | bytes 12296 | tf_op jit(solution)/shard_map/ppermute | solution.py:178
  190.5 5.1 %collective-permute-start.7 = (f32[2,2,256]{2,1,0:T(2,128)S(1)}, f32[2,2,256]{2,1,0:T(2,128)S(1)}, u32[]{:S(2)}, u32[]{:S(2)}) collective-permute-start(f32[2,2,256]{2,1,0:T(2,128)S(1)} %add.261), channel_id=1, source_target_pairs={{0,2},{1,3},{2,0},{3,1},{4,6},{5,7},{6,4},{7,5},{8,10},{9,11},{10,... | collective-permute-start | bytes 12296 | tf_op jit(solution)/shard_map/ppermute | solution.py:178

commit v4 on v2

--- a/solution.py
+++ b/solution.py
@@ -43,6 +43,8 @@
     weight_part = jnp.transpose(weight_one, (1, 0, 2)).reshape(cols_dev, 2 * hidden_width)
     weight_part = jnp.broadcast_to(weight_part[None], (feat_devs, cols_dev, 2 * hidden_width))
     outgoing_one = jnp.concatenate([block_part, self_part, weight_part], axis=2)
+    lanes = 128
+    outgoing_one = outgoing_one.reshape(feat_devs, -1, lanes)
     incoming_one = lax.all_to_all(outgoing_one, "feat", split_axis=0, concat_axis=0, tiled=True)
     gathered = incoming_one.reshape(feat_devs * cols_dev, -1)
     block_x = gathered[:, :span_width]
@@ -114,10 +116,12 @@
         jnp.einsum("rk,hk->rh", slope_two, weight_two[1], preferred_element_type=jnp.float32)
         / fanout_two
     )
+    agg_high = back_agg.astype(jnp.bfloat16)
+    agg_low = (back_agg - agg_high.astype(jnp.float32)).astype(jnp.bfloat16)
+    tallies_bf = tallies_two.astype(jnp.bfloat16)
     grad_table = jnp.einsum(
-        "dr,dh->rh", tallies_two, back_agg, precision=lax.Precision.HIGHEST,
-        preferred_element_type=jnp.float32,
-    )
+        "dr,dh->rh", tallies_bf, agg_high, preferred_element_type=jnp.float32
+    ) + jnp.einsum("dr,dh->rh", tallies_bf, agg_low, preferred_element_type=jnp.float32)
     returned = lax.all_to_all(
         grad_table[node_count:].reshape(peers, capacity, hidden_width).astype(jnp.bfloat16),
         "feat",
@@ -144,10 +148,10 @@
     outgoing_grad = jnp.concatenate([one_part, two_part], axis=1)
     incoming_grad = lax.all_to_all(outgoing_grad, "feat", split_axis=0, concat_axis=0, tiled=True)
     feat_summed = jnp.sum(incoming_grad, axis=0)
-    rep_copies = jnp.broadcast_to(feat_summed[None], (rep_devs,) + feat_summed.shape)
-    reduced = jnp.sum(
-        lax.all_to_all(rep_copies, "rep", split_axis=0, concat_axis=0, tiled=True), axis=0
-    )
+    reduced = feat_summed
+    for bit in range(rep_devs.bit_length() - 1):
+        pairs = [(i, i ^ (1 << bit)) for i in range(rep_devs)]
+        reduced = reduced + lax.ppermute(reduced, "rep", pairs)
     one_size = one_part.shape[1]
     grad_one = reduced[:one_size].reshape(2, cols_dev, hidden_width)
     two_piece = reduced[one_size:]

time: 193 us -> 194 us (level)
  blocking collectives: 37.3 us -> 28.9 us
  starting transfers between devices: 33.1 us -> 38.3 us
  waiting for transfers between devices: 87.6 us -> 91.4 us
    all_to_all x1 -> x0, blocking collectives: 8.37 us -> none  [on_device(): lax.all_to_all(rep_copies, 'rep', split_axis=0, concat_axis=0, tiled=True)]
    ppermute x0 -> x2, starting transfers between devices: none -> 4.28 us  [on_device(): reduced = reduced + lax.ppermute(reduced, 'rep', pairs)]
    ppermute x0 -> x2, waiting for transfers between devices: none -> 2.4 us  [on_device(): reduced = reduced + lax.ppermute(reduced, 'rep', pairs)]
    dot_general x1 -> x2, matrix products: 6.53 us -> 6.68 us  [the longest x1 3.41 us: on_device(): jnp.einsum('dr,dh->rh', tallies_bf, agg_low, preferred_element_type=jnp.f...]
  transfers between devices with their start and end apart: 4 -> 6, of which waited for: 4 -> 6; matrix products, arithmetic and copies ran while one was open for 1% -> 1% of each run, Pallas kernels for 0% -> 0%
where the time goes in v4:
time: 194 us
  waiting for transfers between devices  91.4 us (47%)
  starting transfers between devices  38.3 us (20%)
  blocking collectives  28.9 us (15%)
  matrix products  20 us (10%)
  local copies, waits for them, and re-layouts  11.1 us (6%)
  other arithmetic  3.13 us (2%)
    all_to_all x1, blocking collectives, on_device(): lax.all_to_all(outgoing_grad, 'feat', split_axis=0, concat_axis=0, tiled=...  28.9 us
    all_to_all x1, waiting for transfers between devices, on_device(): lax.all_to_all(outgoing.reshape(peers, capacity, hidden_width), 'feat', s...  28.3 us
    all_to_all x1, waiting for transfers between devices, on_device(): lax.all_to_all(grad_table[node_count:].reshape(peers, capacity, hidden_wi...  27.8 us
    all_to_all x1, waiting for transfers between devices, on_device(): lax.all_to_all(two_copies, 'feat', split_axis=0, concat_axis=0, tiled=True)  16.7 us
    all_to_all x1, waiting for transfers between devices, on_device(): lax.all_to_all(outgoing_one, 'feat', split_axis=0, concat_axis=0, tiled=T...  16.2 us
    all_to_all x1, starting transfers between devices, on_device(): lax.all_to_all(outgoing_one, 'feat', split_axis=0, concat_axis=0, tiled=T...  13 us
    all_to_all x1, starting transfers between devices, on_device(): lax.all_to_all(two_copies, 'feat', split_axis=0, concat_axis=0, tiled=True)  8.52 us
    all_to_all x1, starting transfers between devices, on_device(): lax.all_to_all(outgoing.reshape(peers, capacity, hidden_width), 'feat', s...  6.3 us
  transfers between devices with their start and end apart: 6, of which 6 were waited for; matrix products, arithmetic and copies ran while one was open for 1% of the time, Pallas kernels for 0%

profile of v4, /device:TPU:1, one launch (start us, length us, event | category | flops | bytes accessed | tf_op | source)
XLA Modules:
  0.0 193.8 jit_solution(9260710450670400820)
XLA Ops:
  0.7 0.9 copy.44
  1.6 0.1 copy.23
  1.7 0.9 slice.187
  2.6 0.1 broadcast_in_dim.20
  2.8 0.8 broadcast_in_dim.22
  3.5 0.4 pad_maximum_fusion.2
  3.9 1.1 reshape.177
  5.0 13.0 %all-to-all-start = ((bf16[64,28,128]{2,1,0:T(8,128)(2,1)}), bf16[64,28,128]{2,1,0:T(8,128)(2,1)S(1)}, u32[]{:S(2)}, u32[]{:S(2)}) async-start(bf16[64,28,128]{2,1,0:T(8,128)(2,1)} %reshape.177), calls=%async_computation | async-start | bytes 1048576 | tf_op jit(solution)/shard_map/all_to_all | solution.py:48
  18.4 0.7 dynamic-slice_subtract_fusion
  19.1 16.2 %all-to-all-done = bf16[64,28,128]{2,1,0:T(8,128)(2,1)S(1)} async-done(((bf16[64,28,128]{2,1,0:T(8,128)(2,1)}), bf16[64,28,128]{2,1,0:T(8,128)(2,1)S(1)}, u32[]{:S(2)}, u32[]{:S(2)}) %all-to-all-start) | async-done | bytes 458784 | tf_op jit(solution)/shard_map/all_to_all | solution.py:48
  35.3 0.5 reshape.178
  35.9 0.2 fusion.66
  36.1 0.2 fusion.58
  36.3 2.2 %fusion.21 = bf16[128,256]{1,0:T(8,128)(2,1)S(1)} fusion(s32[256]{0:T(256)S(1)} %bitcast.107, s32[256]{0:T(256)S(1)} %bitcast.108, s32[256]{0:T(256)S(1)} %bitcast.109, s32[256]{0:T(256)S(1)} %bitcast.110, s32[256]{0:T(256)S(1)} %bitcast.111, s32[256]{0:T(256)S(1)} %bitcast.112, s32[256]{0:T(256)S(1)} %bitcast.113, s32[256]{0:T(256)S(1)} %bitcast.114, ...), kind=kOutput, calls=%fused_computation.36 | convolution fusion | flops 78970880 | bytes 343040 | tf_op jit(solution)/shard_map/fs,vs->fv/dot_general | solution.py:62
  38.5 0.3 fusion.42
  38.8 2.7 %convolution_convert_fusion = bf16[2048,256]{1,0:T(8,128)(2,1)} fusion(bf16[256,256]{1,0:T(8,128)(2,1)S(1)} %get-tuple-element.32, s32[2048]{0:T(1024)S(1)} %eq.342, pred[2048]{0:T(1024)(128)(4,1)S(1)} %lt.25), kind=kOutput, calls=%fused_computation.1 | convolution fusion | flops 270008320 | bytes 1189888 | tf_op jit(solution)/shard_map/ji,ih->jh/dot_general | solution.py:77
  41.5 6.3 %all-to-all-start.1 = ((bf16[64,32,256]{2,1,0:T(8,128)(2,1)}), bf16[64,32,256]{2,1,0:T(8,128)(2,1)S(1)}, u32[]{:S(2)}, u32[]{:S(2)}) async-start(bf16[64,32,256]{2,1,0:T(8,128)(2,1)} %bitcast.36), calls=%async_computation.1 | async-start | bytes 2097152 | tf_op jit(solution)/shard_map/all_to_all | solution.py:80
  47.8 0.2 fusion.52
  48.0 28.3 %all-to-all-done.1 = bf16[64,32,256]{2,1,0:T(8,128)(2,1)S(1)} async-done(((bf16[64,32,256]{2,1,0:T(8,128)(2,1)}), bf16[64,32,256]{2,1,0:T(8,128)(2,1)S(1)}, u32[]{:S(2)}, u32[]{:S(2)}) %all-to-all-start.1) | async-done | bytes 1048608 | tf_op jit(solution)/shard_map/all_to_all | solution.py:80
  76.3 3.2 %fusion.18 = bf16[256,256]{1,0:T(8,128)(2,1)S(1)} fusion(bf16[2048,256]{1,0:T(8,128)(2,1)S(1)} %bitcast.97, bf16[256,256]{1,0:T(8,128)(2,1)S(1)} %get-tuple-element.32, s32[256]{0:T(256)S(1)} %bitcast.145, s32[256]{0:T(256)S(1)} %bitcast.148, s32[256]{0:T(256)S(1)} %bitcast.124, s32[256]{0:T(256)S(1)} %bitcast.127, s32[256]{0:T(256)S(1)} %bitcast.130, ...), kind=kOutput, calls=%fused_computation.34 | convolution fusion | flops 322174976 | bytes 1320960 | tf_op jit(solution)/shard_map/dr,rh->dh/dot_general | solution.py:94
  79.4 1.0 fusion.46
  80.4 0.2 convolution_multiply_fusion
  80.6 3.3 %fusion.60 = f32[2304,256]{1,0:T(8,128)S(1)} fusion(f32[256,256]{1,0:T(8,128)S(1)} %convolution_multiply_fusion, s32[256]{0:T(256)S(1)} %bitcast.146, s32[256]{0:T(256)S(1)} %bitcast.149, s32[256]{0:T(256)S(1)} %bitcast.125, s32[256]{0:T(256)S(1)} %bitcast.128, s32[256]{0:T(256)S(1)} %bitcast.131, s32[256]{0:T(256)S(1)} %bitcast.134, ...), kind=kOutput, calls=%fused_computation.103 | convolution fusion | flops 319750144 | bytes 2631680 | tf_op jit(solution)/shard_map/dr,dh->rh/dot_general | solution.py:122
  83.9 3.4 %convolution_add_fusion = f32[2304,256]{1,0:T(8,128)S(1)} fusion(f32[2304,256]{1,0:T(8,128)S(1)} %fusion.60, f32[256,256]{1,0:T(8,128)S(1)} %convolution_multiply_fusion, s32[256]{0:T(256)S(1)} %bitcast.147, s32[256]{0:T(256)S(1)} %bitcast.150, s32[256]{0:T(256)S(1)} %bitcast.126, s32[256]{0:T(256)S(1)} %bitcast.129, s32[256]{0:T(256)S(1)} %bitcast.132, ...), kind=kOutput, calls=%fused_computation | convolution fusion | flops 320536576 | bytes 4990976 | tf_op jit(solution)/shard_map/dr,dh->rh/dot_general | solution.py:124
  87.3 1.4 copy-done
  88.7 1.1 slice.236
  89.8 6.2 %all-to-all-start.2 = ((bf16[64,32,256]{2,1,0:T(8,128)(2,1)}), bf16[64,32,256]{2,1,0:T(8,128)(2,1)S(1)}, u32[]{:S(2)}, u32[]{:S(2)}) async-start(bf16[64,32,256]{2,1,0:T(8,128)(2,1)} %bitcast.42), calls=%async_computation.2 | async-start | bytes 2097152 | tf_op jit(solution)/shard_map/all_to_all | solution.py:125
  96.1 0.2 convolution_bitcast_fusion.1
  96.4 0.2 convolution_bitcast_fusion
  96.7 27.8 %all-to-all-done.2 = bf16[64,32,256]{2,1,0:T(8,128)(2,1)S(1)} async-done(((bf16[64,32,256]{2,1,0:T(8,128)(2,1)}), bf16[64,32,256]{2,1,0:T(8,128)(2,1)S(1)}, u32[]{:S(2)}, u32[]{:S(2)}) %all-to-all-start.2) | async-done | bytes 1048608 | tf_op jit(solution)/shard_map/all_to_all | solution.py:125
  124.6 1.5 fusion.14
  126.1 1.2 fusion.17
  127.3 0.2 fusion.62
  127.5 0.2 fusion.71
  127.9 0.2 reshape.182
  128.2 0.5 all_to_all.22
  128.8 28.9 %all_to_all.30 = f32[64,1,3072]{2,1,0:T(1,128)S(1)} all-to-all(f32[64,1,3072]{2,1,0:T(1,128)S(1)} %all_to_all.22), channel_id=1, replica_groups=mesh['feat'=64,'rep'=4] {'feat'}, dimensions={0} | all-to-all | bytes 1572864 | tf_op jit(solution)/shard_map/all_to_all | solution.py:149
  157.7 0.5 reduce_sum.9
  158.1 1.4 collective-permute-start
  159.5 1.3 collective-permute-done
  160.8 2.9 %collective-permute-start.1 = (f32[3072]{0:T(1024)S(1)}, f32[3072]{0:T(1024)S(1)}, u32[]{:S(2)}, u32[]{:S(2)}) collective-permute-start(f32[3072]{0:T(1024)S(1)} %add.123), channel_id=1, source_target_pairs={{0,2},{1,3},{2,0},{3,1},{4,6},{5,7},{6,4},{7,5},{8,10},{9,11},{10,... | collective-permute-start | bytes 36872 | tf_op jit(solution)/shard_map/ppermute | solution.py:154
  163.7 1.1 collective-permute-done.1
  164.8 1.1 broadcast_in_dim.24
  165.9 8.5 %all-to-all-start.4 = ((f32[64,1,2048]{2,1,0:T(1,128)}), f32[64,1,2048]{2,1,0:T(1,128)S(1)}, u32[]{:S(2)}, u32[]{:S(2)}) async-start(f32[64,1,2048]{2,1,0:T(1,128)} %broadcast_in_dim.24), calls=%async_computation.4 | async-start | bytes 1048576 | tf_op jit(solution)/shard_map/all_to_all | solution.py:159
  174.4 0.6 slice.185
  175.0 16.7 %all-to-all-done.4 = f32[64,1,2048]{2,1,0:T(1,128)S(1)} async-done(((f32[64,1,2048]{2,1,0:T(1,128)}), f32[64,1,2048]{2,1,0:T(1,128)S(1)}, u32[]{:S(2)}, u32[]{:S(2)}) %all-to-all-start.4) | async-done | bytes 524320 | tf_op jit(solution)/shard_map/all_to_all | solution.py:159
  191.7 1.2 reduce.1
  193.0 0.9 reshape.184
  (30 shorter events, 0.9 us)
Async XLA Ops:
  0.6 17.4 %copy-start.4 = (s32[1,1,64]{2,1,0:T(1,128)S(1)}, s32[1,1,64]{2,1,0:T(1,128)}, u32[]{:S(2)}) copy-start(s32[1,1,64]{2,1,0:T(1,128)} %param.13) | copy-start | bytes 772
  0.6 17.6 %copy-start.2 = (s32[1,1,64,32]{2,3,1,0:T(8,128)S(1)}, s32[1,1,64,32]{2,3,1,0:T(8,128)}, u32[]{:S(2)}) copy-start(s32[1,1,64,32]{2,3,1,0:T(8,128)} %param.12) | copy-start | bytes 24580
  5.0 30.3 %all-to-all-start = ((bf16[64,28,128]{2,1,0:T(8,128)(2,1)}), bf16[64,28,128]{2,1,0:T(8,128)(2,1)S(1)}, u32[]{:S(2)}, u32[]{:S(2)}) async-start(bf16[64,28,128]{2,1,0:T(8,128)(2,1)} %reshape.177), calls=%async_computation | async-start | bytes 1048576 | tf_op jit(solution)/shard_map/all_to_all | solution.py:48
  38.5 9.3 %copy-start.3 = (s32[1,10,256]{2,0,1:T(1,128)S(1)}, s32[1,10,256]{2,0,1:T(1,128)}, u32[]{:S(2)}) copy-start(s32[1,10,256]{2,0,1:T(1,128)} %param.14) | copy-start | bytes 30724
  38.5 9.3 %copy-start.1 = (bf16[2,256,256]{2,1,0:T(8,128)(2,1)S(1)}, bf16[2,256,256]{2,1,0:T(8,128)(2,1)}, u32[]{:S(2)}) copy-start(bf16[2,256,256]{2,1,0:T(8,128)(2,1)} %param.11) | copy-start | bytes 786436
  41.5 34.8 %all-to-all-start.1 = ((bf16[64,32,256]{2,1,0:T(8,128)(2,1)}), bf16[64,32,256]{2,1,0:T(8,128)(2,1)S(1)}, u32[]{:S(2)}, u32[]{:S(2)}) async-start(bf16[64,32,256]{2,1,0:T(8,128)(2,1)} %bitcast.36), calls=%async_computation.1 | async-start | bytes 2097152 | tf_op jit(solution)/shard_map/all_to_all | solution.py:80
  76.3 3.2 %copy-start.5 = (bf16[1,256,256]{2,1,0:T(8,128)(2,1)S(1)}, bf16[1,256,256]{2,1,0:T(8,128)(2,1)}, u32[]{:S(2)}) copy-start(bf16[1,256,256]{2,1,0:T(8,128)(2,1)} %param.15) | copy-start | bytes 393220
  87.3 1.4 copy-start
  89.8 34.7 %all-to-all-start.2 = ((bf16[64,32,256]{2,1,0:T(8,128)(2,1)}), bf16[64,32,256]{2,1,0:T(8,128)(2,1)S(1)}, u32[]{:S(2)}, u32[]{:S(2)}) async-start(bf16[64,32,256]{2,1,0:T(8,128)(2,1)} %bitcast.42), calls=%async_computation.2 | async-start | bytes 2097152 | tf_op jit(solution)/shard_map/all_to_all | solution.py:125
  158.1 2.6 %collective-permute-start = (f32[3072]{0:T(1024)S(1)}, f32[3072]{0:T(1024)S(1)}, u32[]{:S(2)}, u32[]{:S(2)}) collective-permute-start(f32[3072]{0:T(1024)S(1)} %reduce_sum.9), channel_id=1, source_target_pairs={{0,1},{1,0},{2,3},{3,2},{4,5},{5,4},{6,7},{7,6},{8,9},{9,8},{10,11... | collective-permute-start | bytes 36872 | tf_op jit(solution)/shard_map/ppermute | solution.py:154
  160.8 4.0 %collective-permute-start.1 = (f32[3072]{0:T(1024)S(1)}, f32[3072]{0:T(1024)S(1)}, u32[]{:S(2)}, u32[]{:S(2)}) collective-permute-start(f32[3072]{0:T(1024)S(1)} %add.123), channel_id=1, source_target_pairs={{0,2},{1,3},{2,0},{3,1},{4,6},{5,7},{6,4},{7,5},{8,10},{9,11},{10,... | collective-permute-start | bytes 36872 | tf_op jit(solution)/shard_map/ppermute | solution.py:154
  165.9 25.8 %all-to-all-start.4 = ((f32[64,1,2048]{2,1,0:T(1,128)}), f32[64,1,2048]{2,1,0:T(1,128)S(1)}, u32[]{:S(2)}, u32[]{:S(2)}) async-start(f32[64,1,2048]{2,1,0:T(1,128)} %broadcast_in_dim.24), calls=%async_computation.4 | async-start | bytes 1048576 | tf_op jit(solution)/shard_map/all_to_all | solution.py:159

commit v5 on v2

--- a/solution.py
+++ b/solution.py
@@ -150,11 +150,11 @@
     )
     one_size = one_part.shape[1]
     grad_one = reduced[:one_size].reshape(2, cols_dev, hidden_width)
-    two_piece = reduced[one_size:]
+    two_piece = reduced[one_size:].astype(jnp.bfloat16)
     two_copies = jnp.broadcast_to(two_piece[None], (feat_devs,) + two_piece.shape)
     grad_two = lax.all_to_all(
         two_copies, "feat", split_axis=0, concat_axis=0, tiled=True
-    ).reshape(local_two.shape)
+    ).astype(jnp.float32).reshape(local_two.shape)
     return (hidden_two[None], grad_one, grad_two)
 
 

time: 193 us -> 191 us (0.990)
  waiting for transfers between devices: 87.6 us -> 82.3 us
  other arithmetic: 3.96 us -> 6.3 us
    all_to_all x1, waiting for transfers between devices: 16.7 us -> 11.4 us  [on_device(): lax.all_to_all(two_copies, 'feat', split_axis=0, concat_axis=0, tiled=True)]
    broadcast_in_dim x0 -> x1, other arithmetic: none -> 2.15 us  [on_device(): jnp.broadcast_to(two_piece[None], (feat_devs,) + two_piece.shape)]
where the time goes in v5:
time: 191 us; the launch traced here: 190 us
  waiting for transfers between devices  82.3 us (43%)
  blocking collectives  37.3 us (20%)
  starting transfers between devices  33.1 us (17%)
  matrix products  19.9 us (10%)
  local copies, waits for them, and re-layouts  10.4 us (5%)
  other arithmetic  6.3 us (3%)
    all_to_all x1, blocking collectives, on_device(): lax.all_to_all(outgoing_grad, 'feat', split_axis=0, concat_axis=0, tiled=...  28.9 us
    all_to_all x1, waiting for transfers between devices, on_device(): lax.all_to_all(outgoing.reshape(peers, capacity, hidden_width), 'feat', s...  28.3 us
    all_to_all x1, waiting for transfers between devices, on_device(): lax.all_to_all(grad_table[node_count:].reshape(peers, capacity, hidden_wi...  27.8 us
    all_to_all x1, waiting for transfers between devices, on_device(): lax.all_to_all(outgoing_one, 'feat', split_axis=0, concat_axis=0, tiled=T...  14.8 us
    all_to_all x1, starting transfers between devices, on_device(): lax.all_to_all(outgoing_one, 'feat', split_axis=0, concat_axis=0, tiled=T...  13 us
    all_to_all x1, waiting for transfers between devices, on_device(): lax.all_to_all(two_copies, 'feat', split_axis=0, concat_axis=0, tiled=True)  11.4 us
    all_to_all x1, blocking collectives, on_device(): lax.all_to_all(rep_copies, 'rep', split_axis=0, concat_axis=0, tiled=True)  8.37 us
    all_to_all x1, starting transfers between devices, on_device(): lax.all_to_all(two_copies, 'feat', split_axis=0, concat_axis=0, tiled=True)  7.65 us
  transfers between devices with their start and end apart: 4, of which 4 were waited for; matrix products, arithmetic and copies ran while one was open for 1% of the time, Pallas kernels for 0%

profile of v5, /device:TPU:1, one launch (start us, length us, event | category | flops | bytes accessed | tf_op | source)
XLA Modules:
  0.0 190.3 jit_solution(11861886544086874998)
XLA Ops:
  0.7 0.9 copy.76
  1.6 0.1 copy.60
  1.7 0.9 slice.188
  2.6 0.1 broadcast_in_dim.12
  2.8 0.8 broadcast_in_dim.28
  3.5 1.2 pad_maximum_fusion.2
  4.7 13.0 %all-to-all-start = ((bf16[64,2,1792]{2,1,0:T(2,128)(2,1)}), bf16[64,2,1792]{2,1,0:T(2,128)(2,1)S(1)}, u32[]{:S(2)}, u32[]{:S(2)}) async-start(bf16[64,2,1792]{2,1,0:T(2,128)(2,1)} %pad_maximum_fusion.2), calls=%async_computation | async-start | bytes 917504 | tf_op jit(solution)/shard_map/all_to_all | solution.py:46
  18.0 0.7 dynamic-slice_subtract_fusion
  18.8 14.8 %all-to-all-done = bf16[64,2,1792]{2,1,0:T(2,128)(2,1)S(1)} async-done(((bf16[64,2,1792]{2,1,0:T(2,128)(2,1)}), bf16[64,2,1792]{2,1,0:T(2,128)(2,1)S(1)}, u32[]{:S(2)}, u32[]{:S(2)}) %all-to-all-start) | async-done | bytes 458784 | tf_op jit(solution)/shard_map/all_to_all | solution.py:46
  33.6 0.2 reshape.180
  33.8 0.1 copy.62
  33.9 0.2 fusion.64
  34.1 2.2 %fusion.27 = bf16[128,256]{1,0:T(8,128)(2,1)S(1)} fusion(s32[256]{0:T(256)S(1)} %bitcast.113, s32[256]{0:T(256)S(1)} %bitcast.114, s32[256]{0:T(256)S(1)} %bitcast.115, s32[256]{0:T(256)S(1)} %bitcast.116, s32[256]{0:T(256)S(1)} %bitcast.117, s32[256]{0:T(256)S(1)} %bitcast.118, s32[256]{0:T(256)S(1)} %bitcast.119, s32[256]{0:T(256)S(1)} %bitcast.120, ...), kind=kOutput, calls=%fused_computation.37 | convolution fusion | flops 78970880 | bytes 343040 | tf_op jit(solution)/shard_map/fs,vs->fv/dot_general | solution.py:60
  36.3 0.3 fusion.48
  36.6 2.7 %convolution_convert_fusion = bf16[2048,256]{1,0:T(8,128)(2,1)} fusion(bf16[256,256]{1,0:T(8,128)(2,1)S(1)} %get-tuple-element.30, s32[2048]{0:T(1024)S(1)} %eq.342, pred[2048]{0:T(1024)(128)(4,1)S(1)} %lt.25), kind=kOutput, calls=%fused_computation | convolution fusion | flops 270008320 | bytes 1189888 | tf_op jit(solution)/shard_map/ji,ih->jh/dot_general | solution.py:75
  39.3 6.3 %all-to-all-start.1 = ((bf16[64,32,256]{2,1,0:T(8,128)(2,1)}), bf16[64,32,256]{2,1,0:T(8,128)(2,1)S(1)}, u32[]{:S(2)}, u32[]{:S(2)}) async-start(bf16[64,32,256]{2,1,0:T(8,128)(2,1)} %bitcast.37), calls=%async_computation.1 | async-start | bytes 2097152 | tf_op jit(solution)/shard_map/all_to_all | solution.py:78
  45.6 0.2 fusion.58
  45.8 28.3 %all-to-all-done.1 = bf16[64,32,256]{2,1,0:T(8,128)(2,1)S(1)} async-done(((bf16[64,32,256]{2,1,0:T(8,128)(2,1)}), bf16[64,32,256]{2,1,0:T(8,128)(2,1)S(1)}, u32[]{:S(2)}, u32[]{:S(2)}) %all-to-all-start.1) | async-done | bytes 1048608 | tf_op jit(solution)/shard_map/all_to_all | solution.py:78
  74.1 3.2 %fusion.21 = bf16[256,256]{1,0:T(8,128)(2,1)S(1)} fusion(bf16[2048,256]{1,0:T(8,128)(2,1)S(1)} %bitcast.101, bf16[256,256]{1,0:T(8,128)(2,1)S(1)} %get-tuple-element.30, s32[256]{0:T(256)S(1)} %bitcast.143, s32[256]{0:T(256)S(1)} %bitcast.145, s32[256]{0:T(256)S(1)} %bitcast.129, s32[256]{0:T(256)S(1)} %bitcast.131, s32[256]{0:T(256)S(1)} %bitcast.133, ...), kind=kOutput, calls=%fused_computation.34 | convolution fusion | flops 322174976 | bytes 1320960 | tf_op jit(solution)/shard_map/dr,rh->dh/dot_general | solution.py:92
  77.3 1.0 fusion.52
  78.3 0.2 convolution_multiply_fusion
  78.5 6.5 %fusion.10 = f32[2304,256]{1,0:T(8,128)S(1)} fusion(f32[256,256]{1,0:T(8,128)S(1)} %convolution_multiply_fusion, s32[256]{0:T(256)S(1)} %bitcast.144, s32[256]{0:T(256)S(1)} %bitcast.146, s32[256]{0:T(256)S(1)} %bitcast.130, s32[256]{0:T(256)S(1)} %bitcast.132, s32[256]{0:T(256)S(1)} %bitcast.134, s32[256]{0:T(256)S(1)} %bitcast.136, s32[256]{0:T(256)S(1)} %bitcast.138, ...), kind=kOutput, calls=%fused_computation.23 | convolution fusion | flops 1829044224 | bytes 2631680 | tf_op jit(solution)/shard_map/dr,dh->rh/dot_general | solution.py:117
  85.0 1.4 copy-done
  86.4 1.1 slice.242
  87.5 6.2 %all-to-all-start.2 = ((bf16[64,32,256]{2,1,0:T(8,128)(2,1)}), bf16[64,32,256]{2,1,0:T(8,128)(2,1)S(1)}, u32[]{:S(2)}, u32[]{:S(2)}) async-start(bf16[64,32,256]{2,1,0:T(8,128)(2,1)} %bitcast.43), calls=%async_computation.2 | async-start | bytes 2097152 | tf_op jit(solution)/shard_map/all_to_all | solution.py:121
  93.8 0.2 convolution_bitcast_fusion.1
  94.1 0.2 convolution_bitcast_fusion
  94.4 27.8 %all-to-all-done.2 = bf16[64,32,256]{2,1,0:T(8,128)(2,1)S(1)} async-done(((bf16[64,32,256]{2,1,0:T(8,128)(2,1)}), bf16[64,32,256]{2,1,0:T(8,128)(2,1)S(1)}, u32[]{:S(2)}, u32[]{:S(2)}) %all-to-all-start.2) | async-done | bytes 1048608 | tf_op jit(solution)/shard_map/all_to_all | solution.py:121
  122.3 1.5 fusion.13
  123.8 1.2 fusion.26
  125.0 0.2 fusion.65
  125.1 0.2 fusion.73
  125.5 0.1 maximum_bitcast_fusion
  125.6 0.2 reshape.184
  125.9 0.5 all_to_all.26
  126.4 28.9 %all_to_all.36 = f32[64,1,3072]{2,1,0:T(1,128)S(1)} all-to-all(f32[64,1,3072]{2,1,0:T(1,128)S(1)} %all_to_all.26), channel_id=1, replica_groups=mesh['feat'=64,'rep'=4] {'feat'}, dimensions={0} | all-to-all | bytes 1572864 | tf_op jit(solution)/shard_map/all_to_all | solution.py:145
  155.3 0.5 reduce_sum.18
  155.8 8.4 %all_to_all.37 = f32[4,1,3072]{2,1,0:T(1,128)S(1)} all-to-all(f32[4,1,3072]{2,1,0:T(1,128)S(1)} %broadcast_in_dim.30), channel_id=1, replica_groups=mesh['feat'=64,'rep'=4] {'rep'}, dimensions={0} | all-to-all | bytes 98304 | tf_op jit(solution)/shard_map/all_to_all | solution.py:149
  164.3 0.3 broadcast_in_dim.31
  164.6 0.5 broadcast.48
  165.1 2.2 %reduce.4 = bf16[64,2048]{1,0:T(8,128)(2,1)S(1)} reduce(bf16[64,1,2048]{2,1,0:T(2,128)(2,1)S(1)} %broadcast_in_dim.31, bf16[]{:T(256)} %broadcast.48), dimensions={1}, to_apply=%broadcast_in_dim.31.reduce_sub_computation | reduce | bytes 524290 | tf_op jit(solution)/shard_map/broadcast_in_dim | solution.py:154
  167.2 0.9 reshape.190
  168.1 7.6 %all-to-all-start.5 = ((bf16[64,2,1024]{2,1,0:T(2,128)(2,1)}), bf16[64,2,1024]{2,1,0:T(2,128)(2,1)S(1)}, u32[]{:S(2)}, u32[]{:S(2)}) async-start(bf16[64,2,1024]{2,1,0:T(2,128)(2,1)} %reshape.190), calls=%async_computation.5 | async-start | bytes 524288 | tf_op jit(solution)/shard_map/all_to_all | solution.py:155
  175.8 0.6 slice.186
  176.4 11.4 %all-to-all-done.5 = bf16[64,2,1024]{2,1,0:T(2,128)(2,1)S(1)} async-done(((bf16[64,2,1024]{2,1,0:T(2,128)(2,1)}), bf16[64,2,1024]{2,1,0:T(2,128)(2,1)S(1)}, u32[]{:S(2)}, u32[]{:S(2)}) %all-to-all-start.5) | async-done | bytes 262176 | tf_op jit(solution)/shard_map/all_to_all | solution.py:155
  187.7 0.2 reshape.191
  188.0 1.4 convert_reduce_fusion
  189.4 0.9 reshape.187
  (28 shorter events, 0.9 us)
Async XLA Ops:
  0.6 17.1 %copy-start.4 = (s32[1,1,64]{2,1,0:T(1,128)S(1)}, s32[1,1,64]{2,1,0:T(1,128)}, u32[]{:S(2)}) copy-start(s32[1,1,64]{2,1,0:T(1,128)} %param.13) | copy-start | bytes 772
  0.6 17.2 %copy-start.2 = (s32[1,1,64,32]{2,3,1,0:T(8,128)S(1)}, s32[1,1,64,32]{2,3,1,0:T(8,128)}, u32[]{:S(2)}) copy-start(s32[1,1,64,32]{2,3,1,0:T(8,128)} %param.12) | copy-start | bytes 24580
  4.7 28.9 %all-to-all-start = ((bf16[64,2,1792]{2,1,0:T(2,128)(2,1)}), bf16[64,2,1792]{2,1,0:T(2,128)(2,1)S(1)}, u32[]{:S(2)}, u32[]{:S(2)}) async-start(bf16[64,2,1792]{2,1,0:T(2,128)(2,1)} %pad_maximum_fusion.2), calls=%async_computation | async-start | bytes 917504 | tf_op jit(solution)/shard_map/all_to_all | solution.py:46
  36.3 9.3 %copy-start.3 = (s32[1,10,256]{2,0,1:T(1,128)S(1)}, s32[1,10,256]{2,0,1:T(1,128)}, u32[]{:S(2)}) copy-start(s32[1,10,256]{2,0,1:T(1,128)} %param.14) | copy-start | bytes 30724
  36.3 9.3 %copy-start.1 = (bf16[2,256,256]{2,1,0:T(8,128)(2,1)S(1)}, bf16[2,256,256]{2,1,0:T(8,128)(2,1)}, u32[]{:S(2)}) copy-start(bf16[2,256,256]{2,1,0:T(8,128)(2,1)} %param.11) | copy-start | bytes 786436
  39.3 34.8 %all-to-all-start.1 = ((bf16[64,32,256]{2,1,0:T(8,128)(2,1)}), bf16[64,32,256]{2,1,0:T(8,128)(2,1)S(1)}, u32[]{:S(2)}, u32[]{:S(2)}) async-start(bf16[64,32,256]{2,1,0:T(8,128)(2,1)} %bitcast.37), calls=%async_computation.1 | async-start | bytes 2097152 | tf_op jit(solution)/shard_map/all_to_all | solution.py:78
  74.1 3.2 %copy-start.5 = (bf16[1,256,256]{2,1,0:T(8,128)(2,1)S(1)}, bf16[1,256,256]{2,1,0:T(8,128)(2,1)}, u32[]{:S(2)}) copy-start(bf16[1,256,256]{2,1,0:T(8,128)(2,1)} %param.15) | copy-start | bytes 393220
  85.0 1.4 copy-start
  87.5 34.7 %all-to-all-start.2 = ((bf16[64,32,256]{2,1,0:T(8,128)(2,1)}), bf16[64,32,256]{2,1,0:T(8,128)(2,1)S(1)}, u32[]{:S(2)}, u32[]{:S(2)}) async-start(bf16[64,32,256]{2,1,0:T(8,128)(2,1)} %bitcast.43), calls=%async_computation.2 | async-start | bytes 2097152 | tf_op jit(solution)/shard_map/all_to_all | solution.py:121
  168.1 19.6 %all-to-all-start.5 = ((bf16[64,2,1024]{2,1,0:T(2,128)(2,1)}), bf16[64,2,1024]{2,1,0:T(2,128)(2,1)S(1)}, u32[]{:S(2)}, u32[]{:S(2)}) async-start(bf16[64,2,1024]{2,1,0:T(2,128)(2,1)} %reshape.190), calls=%async_computation.5 | async-start | bytes 524288 | tf_op jit(solution)/shard_map/all_to_all | solution.py:155

commit v6 on v5

--- a/solution.py
+++ b/solution.py
@@ -32,6 +32,32 @@
     span_count = sources // span_width
     nodes_per_span = BLOCK_NODES // node_count
 
+    my_index = lax.dynamic_slice_in_dim(index_one, me * node_count, node_count, axis=1)
+    block_start = (me * node_count) // BLOCK_NODES * span_width
+    relative = my_index - block_start
+    positions = lax.broadcasted_iota(jnp.int32, (node_count, span_width), 1)
+    tallies = jnp.zeros((node_count, span_width), jnp.float32)
+    for sample in range(fanout_one):
+        tallies = tallies + (relative[sample][:, None] == positions).astype(jnp.float32)
+    tallies = tallies.astype(jnp.bfloat16)
+    send_slots = send_rows[0, 0]
+    counts = halo_count[0, 0]
+    peers, capacity = send_slots.shape
+    live_slots = lax.broadcasted_iota(jnp.int32, send_slots.shape, 1) < counts[:, None]
+    local_rows = lax.broadcasted_iota(jnp.int32, (peers, capacity, node_count), 2)
+    picks = ((send_slots[:, :, None] == local_rows) & live_slots[:, :, None]).astype(jnp.bfloat16)
+    picks = picks.reshape(peers * capacity, node_count)
+    index_two = neighbors_two[0]
+    fanout_two = index_two.shape[0]
+    seed_rows = index_two.shape[1]
+    table_rows = node_count + peers * capacity
+    rows_two = lax.broadcasted_iota(jnp.int32, (seed_rows, table_rows), 1)
+    tallies_two = jnp.zeros((seed_rows, table_rows), jnp.float32)
+    for sample in range(fanout_two):
+        tallies_two = tallies_two + (index_two[sample][:, None] == rows_two).astype(jnp.float32)
+    tallies_two = tallies_two.astype(jnp.bfloat16)
+    tallies, picks, tallies_two = lax.optimization_barrier((tallies, picks, tallies_two))
+
     block_part = jnp.repeat(
         jnp.transpose(table_x.reshape(cols_dev, span_count, span_width), (1, 0, 2)),
         nodes_per_span,
@@ -49,14 +75,6 @@
     self_x = gathered[:, span_width : span_width + node_count]
     full_weight = gathered[:, span_width + node_count :].reshape(-1, 2, hidden_width)
 
-    my_index = lax.dynamic_slice_in_dim(index_one, me * node_count, node_count, axis=1)
-    block_start = (me * node_count) // BLOCK_NODES * span_width
-    relative = my_index - block_start
-    positions = lax.broadcasted_iota(jnp.int32, (node_count, span_width), 1)
-    tallies = jnp.zeros((node_count, span_width), jnp.float32)
-    for sample in range(fanout_one):
-        tallies = tallies + (relative[sample][:, None] == positions).astype(jnp.float32)
-    tallies = tallies.astype(jnp.bfloat16)
     summed_one = jnp.einsum("fs,vs->fv", block_x, tallies, preferred_element_type=jnp.float32)
     aggregate_one = (summed_one / fanout_one).astype(jnp.bfloat16)
 
@@ -65,13 +83,6 @@
     ) + jnp.einsum("fv,fh->vh", aggregate_one, full_weight[:, 1], preferred_element_type=jnp.float32)
     hidden_one = activate(pre_one).astype(jnp.bfloat16)
 
-    send_slots = send_rows[0, 0]
-    counts = halo_count[0, 0]
-    peers, capacity = send_slots.shape
-    live_slots = lax.broadcasted_iota(jnp.int32, send_slots.shape, 1) < counts[:, None]
-    local_rows = lax.broadcasted_iota(jnp.int32, (peers, capacity, node_count), 2)
-    picks = ((send_slots[:, :, None] == local_rows) & live_slots[:, :, None]).astype(jnp.bfloat16)
-    picks = picks.reshape(peers * capacity, node_count)
     outgoing = jnp.einsum(
         "ji,ih->jh", picks, hidden_one, preferred_element_type=jnp.float32
     ).astype(jnp.bfloat16)
@@ -81,16 +92,8 @@
     table_two = jnp.concatenate(
         [hidden_one, incoming.reshape(feat_devs * capacity, hidden_width)], axis=0
     )
-    index_two = neighbors_two[0]
-    fanout_two = index_two.shape[0]
-    seed_rows = index_two.shape[1]
-    table_rows = table_two.shape[0]
-    rows_two = lax.broadcasted_iota(jnp.int32, (seed_rows, table_rows), 1)
-    tallies_two = jnp.zeros((seed_rows, table_rows), jnp.float32)
-    for sample in range(fanout_two):
-        tallies_two = tallies_two + (index_two[sample][:, None] == rows_two).astype(jnp.float32)
     summed_two = jnp.einsum(
-        "dr,rh->dh", tallies_two.astype(jnp.bfloat16), table_two, preferred_element_type=jnp.float32
+        "dr,rh->dh", tallies_two, table_two, preferred_element_type=jnp.float32
     )
     aggregate_two = (summed_two / fanout_two).astype(jnp.bfloat16)
     pre_two = jnp.dot(hidden_one, weight_two[0], preferred_element_type=jnp.float32) + jnp.dot(
@@ -115,7 +118,7 @@
         / fanout_two
     )
     grad_table = jnp.einsum(
-        "dr,dh->rh", tallies_two, back_agg, precision=lax.Precision.HIGHEST,
+        "dr,dh->rh", tallies_two.astype(jnp.float32), back_agg, precision=lax.Precision.HIGHEST,
         preferred_element_type=jnp.float32,
     )
     returned = lax.all_to_all(

time: 191 us -> 183 us (0.958)
  waiting for transfers between devices: 82.3 us -> 70.5 us
  other arithmetic: 6.3 us -> 14.1 us
  matrix products: 19.9 us -> 12.8 us
  local copies, waits for them, and re-layouts: 10.4 us -> 12.5 us
    all_to_all x1, waiting for transfers between devices: 14.8 us -> 7.63 us  [on_device(): lax.all_to_all(outgoing_one, 'feat', split_axis=0, concat_axis=0, tiled=T...]
    convert_element_type x0 -> x3, other arithmetic: none -> 7.03 us  [the longest x1 3.54 us: on_device(): tallies_two = tallies_two.astype(jnp.bfloat16)]
    dot_general x2, matrix products: 9.69 us -> 3.06 us  [the longest x1 1.7 us: on_device(): jnp.einsum('dr,rh->dh', tallies_two, table_two, preferred_element_type=jn...]
    all_to_all x1, waiting for transfers between devices: 27.8 us -> 23.3 us  [on_device(): lax.all_to_all(grad_table[node_count:].reshape(peers, capacity, hidden_wi...]
  transfers between devices with their start and end apart: 4 -> 4, of which waited for: 4 -> 4; matrix products, arithmetic and copies ran while one was open for 1% -> 8% of each run, Pallas kernels for 0% -> 0%
where the time goes in v6:
time: 183 us; the launch traced here: 182 us
  waiting for transfers between devices  70.5 us (39%)
  blocking collectives  37.3 us (20%)
  starting transfers between devices  33.7 us (18%)
  other arithmetic  14.1 us (8%)
  matrix products  12.8 us (7%)
  local copies, waits for them, and re-layouts  12.5 us (7%)
    all_to_all x1, blocking collectives, on_device(): lax.all_to_all(outgoing_grad, 'feat', split_axis=0, concat_axis=0, tiled=...  28.9 us
    all_to_all x1, waiting for transfers between devices, on_device(): lax.all_to_all(outgoing.reshape(peers, capacity, hidden_width), 'feat', s...  28.2 us
    all_to_all x1, waiting for transfers between devices, on_device(): lax.all_to_all(grad_table[node_count:].reshape(peers, capacity, hidden_wi...  23.3 us
    all_to_all x1, starting transfers between devices, on_device(): lax.all_to_all(outgoing_one, 'feat', split_axis=0, concat_axis=0, tiled=T...  13.1 us
    all_to_all x1, waiting for transfers between devices, on_device(): lax.all_to_all(two_copies, 'feat', split_axis=0, concat_axis=0, tiled=True)  11.4 us
    all_to_all x1, blocking collectives, on_device(): lax.all_to_all(rep_copies, 'rep', split_axis=0, concat_axis=0, tiled=True)  8.37 us
    all_to_all x1, starting transfers between devices, on_device(): lax.all_to_all(two_copies, 'feat', split_axis=0, concat_axis=0, tiled=True)  7.65 us
    all_to_all x1, waiting for transfers between devices, on_device(): lax.all_to_all(outgoing_one, 'feat', split_axis=0, concat_axis=0, tiled=T...  7.63 us
  transfers between devices with their start and end apart: 4, of which 4 were waited for; matrix products, arithmetic and copies ran while one was open for 8% of the time, Pallas kernels for 0%

profile of v6, /device:TPU:1, one launch (start us, length us, event | category | flops | bytes accessed | tf_op | source)
XLA Modules:
  0.0 182.0 jit_solution(15375858356594558302)
XLA Ops:
  0.7 0.9 copy.61
  1.8 0.9 slice.188
  2.8 0.8 broadcast_in_dim.28
  3.5 1.2 pad_maximum_fusion.2
  4.7 13.1 %all-to-all-start = ((bf16[64,2,1792]{2,1,0:T(2,128)(2,1)}), bf16[64,2,1792]{2,1,0:T(2,128)(2,1)}, u32[]{:S(2)}, u32[]{:S(2)}) async-start(bf16[64,2,1792]{2,1,0:T(2,128)(2,1)} %pad_maximum_fusion.2), calls=%async_computation | async-start | bytes 917504 | tf_op jit(solution)/shard_map/all_to_all | solution.py:72
  17.9 0.7 dynamic-slice_subtract_fusion
  19.0 1.5 fusion.1
  20.5 2.0 %add_convert_fusion.1 = bf16[256,1024]{1,0:T(8,128)(2,1)S(1)} fusion(s32[256]{0:T(256)S(1)} %bitcast.115, s32[256]{0:T(256)S(1)} %bitcast.116, s32[256]{0:T(256)S(1)} %bitcast.117, s32[256]{0:T(256)S(1)} %bitcast.118, s32[256]{0:T(256)S(1)} %bitcast.119, s32[256]{0:T(256)S(1)} %bitcast.120, s32[256]{0:T(256)S(1)} %bitcast.121, s32[256]{0:T(256)S(1)} %bitcast.122, ...), kind=kLoop, calls=%fused_computation.33 | loop fusion | flops 11796480 | bytes 539648 | tf_op jit(solution)/shard_map/convert_element_type | solution.py:42
  22.5 3.5 %add_convert_fusion = bf16[256,2304]{1,0:T(8,128)(2,1)S(1)} fusion(s32[256]{0:T(256)S(1)} %bitcast.137, s32[256]{0:T(256)S(1)} %bitcast.138, s32[256]{0:T(256)S(1)} %bitcast.130, s32[256]{0:T(256)S(1)} %bitcast.131, s32[256]{0:T(256)S(1)} %bitcast.132, s32[256]{0:T(256)S(1)} %bitcast.133, s32[256]{0:T(256)S(1)} %bitcast.134, s32[256]{0:T(256)S(1)} %bitcast.135, ...), kind=kLoop, calls=%fused_computation.1 | loop fusion | flops 17694720 | bytes 1189888 | tf_op jit(solution)/shard_map/convert_element_type | solution.py:58
  26.1 7.6 %all-to-all-done = bf16[64,2,1792]{2,1,0:T(2,128)(2,1)} async-done(((bf16[64,2,1792]{2,1,0:T(2,128)(2,1)}), bf16[64,2,1792]{2,1,0:T(2,128)(2,1)}, u32[]{:S(2)}, u32[]{:S(2)}) %all-to-all-start) | async-done | bytes 458784 | tf_op jit(solution)/shard_map/all_to_all | solution.py:72
  33.7 1.2 reshape.175
  34.9 0.3 fusion.15
  35.4 0.2 fusion.32
  35.6 1.0 fusion.16
  36.6 1.4 convolution_convert_fusion
  38.0 6.5 %all-to-all-start.1 = ((bf16[64,32,256]{2,1,0:T(8,128)(2,1)}), bf16[64,32,256]{2,1,0:T(8,128)(2,1)}, u32[]{:S(2)}, u32[]{:S(2)}) async-start(bf16[64,32,256]{2,1,0:T(8,128)(2,1)} %bitcast.37), calls=%async_computation.1 | async-start | bytes 2097152 | tf_op jit(solution)/shard_map/all_to_all | solution.py:89
  44.5 0.2 fusion.26
  44.7 28.2 %all-to-all-done.1 = bf16[64,32,256]{2,1,0:T(8,128)(2,1)} async-done(((bf16[64,32,256]{2,1,0:T(8,128)(2,1)}), bf16[64,32,256]{2,1,0:T(8,128)(2,1)}, u32[]{:S(2)}, u32[]{:S(2)}) %all-to-all-start.1) | async-done | bytes 1048608 | tf_op jit(solution)/shard_map/all_to_all | solution.py:89
  72.9 1.7 fusion.12
  74.7 1.0 fusion.20
  75.6 0.6 copy-done.4
  76.3 0.2 convolution_multiply_fusion
  76.5 1.4 fusion.41
  77.9 1.1 slice.242
  79.0 6.4 %all-to-all-start.2 = ((bf16[64,32,256]{2,1,0:T(8,128)(2,1)}), bf16[64,32,256]{2,1,0:T(8,128)(2,1)}, u32[]{:S(2)}, u32[]{:S(2)}) async-start(bf16[64,32,256]{2,1,0:T(8,128)(2,1)} %bitcast.104), calls=%async_computation.2 | async-start | bytes 2097152 | tf_op jit(solution)/shard_map/all_to_all | solution.py:124
  85.4 1.1 convolution_bitcast_fusion.1
  86.5 1.2 convolution_bitcast_fusion
  87.7 0.8 pad_maximum_fusion.1
  88.5 1.9 %reshape.181 = f32[64,2048]{1,0:T(8,128)} reshape(f32[2,256,256]{2,1,0:T(8,128)} %pad_maximum_fusion.1) | data formatting | bytes 1048576 | tf_op jit(solution)/shard_map/reshape | solution.py:146
  90.5 23.3 %all-to-all-done.2 = bf16[64,32,256]{2,1,0:T(8,128)(2,1)} async-done(((bf16[64,32,256]{2,1,0:T(8,128)(2,1)}), bf16[64,32,256]{2,1,0:T(8,128)(2,1)}, u32[]{:S(2)}, u32[]{:S(2)}) %all-to-all-start.2) | async-done | bytes 1048608 | tf_op jit(solution)/shard_map/all_to_all | solution.py:124
  113.8 1.8 fusion.42
  115.6 0.2 fusion.11
  115.8 1.0 fusion.33
  117.3 0.2 reshape.180
  117.6 0.5 all_to_all.26
  118.1 28.9 %all_to_all.36 = f32[64,1,3072]{2,1,0:T(1,128)S(1)} all-to-all(f32[64,1,3072]{2,1,0:T(1,128)S(1)} %all_to_all.26), channel_id=1, replica_groups=mesh['feat'=64,'rep'=4] {'feat'}, dimensions={0} | all-to-all | bytes 1572864 | tf_op jit(solution)/shard_map/all_to_all | solution.py:148
  147.1 0.5 reduce_sum.18
  147.6 8.4 %all_to_all.37 = f32[4,1,3072]{2,1,0:T(1,128)S(1)} all-to-all(f32[4,1,3072]{2,1,0:T(1,128)S(1)} %broadcast_in_dim.30), channel_id=1, replica_groups=mesh['feat'=64,'rep'=4] {'rep'}, dimensions={0} | all-to-all | bytes 98304 | tf_op jit(solution)/shard_map/all_to_all | solution.py:152
  156.0 0.3 broadcast_in_dim.31
  156.3 0.5 broadcast.45
  156.8 2.2 %reduce.4 = bf16[64,2048]{1,0:T(8,128)(2,1)S(1)} reduce(bf16[64,1,2048]{2,1,0:T(2,128)(2,1)S(1)} %broadcast_in_dim.31, bf16[]{:T(256)} %broadcast.45), dimensions={1}, to_apply=%broadcast_in_dim.31.reduce_sub_computation | reduce | bytes 524290 | tf_op jit(solution)/shard_map/broadcast_in_dim | solution.py:157
  159.0 0.9 reshape.185
  159.8 7.7 %all-to-all-start.5 = ((bf16[64,2,1024]{2,1,0:T(2,128)(2,1)}), bf16[64,2,1024]{2,1,0:T(2,128)(2,1)S(1)}, u32[]{:S(2)}, u32[]{:S(2)}) async-start(bf16[64,2,1024]{2,1,0:T(2,128)(2,1)} %reshape.185), calls=%async_computation.5 | async-start | bytes 524288 | tf_op jit(solution)/shard_map/all_to_all | solution.py:158
  167.5 0.6 slice.186
  168.1 11.4 %all-to-all-done.5 = bf16[64,2,1024]{2,1,0:T(2,128)(2,1)S(1)} async-done(((bf16[64,2,1024]{2,1,0:T(2,128)(2,1)}), bf16[64,2,1024]{2,1,0:T(2,128)(2,1)S(1)}, u32[]{:S(2)}, u32[]{:S(2)}) %all-to-all-start.5) | async-done | bytes 262176 | tf_op jit(solution)/shard_map/all_to_all | solution.py:158
  179.5 0.2 reshape.186
  179.7 1.4 convert_reduce_fusion
  181.1 0.9 reshape.183
  (50 shorter events, 1.4 us)
Async XLA Ops:
  0.6 18.0 %copy-start.12 = (s32[1,1,64,32]{2,3,1,0:T(8,128)S(1)}, s32[1,1,64,32]{2,3,1,0:T(8,128)}, u32[]{:S(2)}) copy-start(s32[1,1,64,32]{2,3,1,0:T(8,128)} %param.12) | copy-start | bytes 24580
  0.6 18.2 %copy-start.14 = (s32[1,1,64]{2,1,0:T(1,128)S(1)}, s32[1,1,64]{2,1,0:T(1,128)}, u32[]{:S(2)}) copy-start(s32[1,1,64]{2,1,0:T(1,128)} %param.13) | copy-start | bytes 772
  1.6 20.9 %copy-start.13 = (s32[1,10,256]{2,0,1:T(1,128)S(1)}, s32[1,10,256]{2,0,1:T(1,128)}, u32[]{:S(2)}) copy-start(s32[1,10,256]{2,0,1:T(1,128)} %param.14) | copy-start | bytes 30724
  4.7 29.0 %all-to-all-start = ((bf16[64,2,1792]{2,1,0:T(2,128)(2,1)}), bf16[64,2,1792]{2,1,0:T(2,128)(2,1)}, u32[]{:S(2)}, u32[]{:S(2)}) async-start(bf16[64,2,1792]{2,1,0:T(2,128)(2,1)} %pad_maximum_fusion.2), calls=%async_computation | async-start | bytes 917504 | tf_op jit(solution)/shard_map/all_to_all | solution.py:72
  26.1 46.9 %copy-start = (bf16[256,2304]{1,0:T(8,128)(2,1)}, bf16[256,2304]{1,0:T(8,128)(2,1)S(1)}, u32[]{:S(2)}) copy-start(bf16[256,2304]{1,0:T(8,128)(2,1)S(1)} %add_convert_fusion) | copy-start | bytes 3538948
  34.9 3.1 %copy-start.2 = (bf16[128,1792]{1,0:T(8,128)(2,1)}, bf16[128,1792]{1,0:T(8,128)(2,1)S(1)}, u32[]{:S(2)}) copy-start(bf16[128,1792]{1,0:T(8,128)(2,1)S(1)} %reshape.175) | copy-start | bytes 1376260
  35.2 2.8 %copy-start.9 = (bf16[128,256]{1,0:T(8,128)(2,1)}, bf16[128,256]{1,0:T(8,128)(2,1)S(1)}, u32[]{:S(2)}) copy-start(bf16[128,256]{1,0:T(8,128)(2,1)S(1)} %fusion.15) | copy-start | bytes 196612
  36.6 7.9 %copy-start.7 = (bf16[2,256,256]{2,1,0:T(8,128)(2,1)S(1)}, bf16[2,256,256]{2,1,0:T(8,128)(2,1)}, u32[]{:S(2)}) copy-start(bf16[2,256,256]{2,1,0:T(8,128)(2,1)} %param.11) | copy-start | bytes 786436
  38.0 34.9 %all-to-all-start.1 = ((bf16[64,32,256]{2,1,0:T(8,128)(2,1)}), bf16[64,32,256]{2,1,0:T(8,128)(2,1)}, u32[]{:S(2)}, u32[]{:S(2)}) async-start(bf16[64,32,256]{2,1,0:T(8,128)(2,1)} %bitcast.37), calls=%async_computation.1 | async-start | bytes 2097152 | tf_op jit(solution)/shard_map/all_to_all | solution.py:89
  44.5 30.1 %copy-start.15 = (bf16[1,256,256]{2,1,0:T(8,128)(2,1)S(1)}, bf16[1,256,256]{2,1,0:T(8,128)(2,1)}, u32[]{:S(2)}) copy-start(bf16[1,256,256]{2,1,0:T(8,128)(2,1)} %param.15) | copy-start | bytes 393220
  74.7 1.0 copy-start.11
  74.7 1.8 %copy-start.1 = (bf16[256,2304]{1,0:T(8,128)(2,1)S(1)}, bf16[256,2304]{1,0:T(8,128)(2,1)}, u32[]{:S(2)}) copy-start(bf16[256,2304]{1,0:T(8,128)(2,1)} %copy-done) | copy-start | bytes 3538948
  75.6 0.6 copy-start.4
  79.0 34.8 %all-to-all-start.2 = ((bf16[64,32,256]{2,1,0:T(8,128)(2,1)}), bf16[64,32,256]{2,1,0:T(8,128)(2,1)}, u32[]{:S(2)}, u32[]{:S(2)}) async-start(bf16[64,32,256]{2,1,0:T(8,128)(2,1)} %bitcast.104), calls=%async_computation.2 | async-start | bytes 2097152 | tf_op jit(solution)/shard_map/all_to_all | solution.py:124
  87.7 27.9 %copy-start.5 = (bf16[256,256]{1,0:T(8,128)(2,1)S(1)}, bf16[256,256]{1,0:T(8,128)(2,1)}, u32[]{:S(2)}) copy-start(bf16[256,256]{1,0:T(8,128)(2,1)} %copy-done.4) | copy-start | bytes 393220
  113.8 1.8 copy-start.6
  113.8 1.8 copy-start.8
  113.8 3.0 %copy-start.10 = (bf16[128,256]{1,0:T(8,128)(2,1)S(1)}, bf16[128,256]{1,0:T(8,128)(2,1)}, u32[]{:S(2)}) copy-start(bf16[128,256]{1,0:T(8,128)(2,1)} %copy-done.9) | copy-start | bytes 196612
  115.6 2.0 %copy-start.3 = (f32[64,2048]{1,0:T(8,128)S(1)}, f32[64,2048]{1,0:T(8,128)}, u32[]{:S(2)}) copy-start(f32[64,2048]{1,0:T(8,128)} %reshape.181) | copy-start | bytes 1572868
  159.8 19.6 %all-to-all-start.5 = ((bf16[64,2,1024]{2,1,0:T(2,128)(2,1)}), bf16[64,2,1024]{2,1,0:T(2,128)(2,1)S(1)}, u32[]{:S(2)}, u32[]{:S(2)}) async-start(bf16[64,2,1024]{2,1,0:T(2,128)(2,1)} %reshape.185), calls=%async_computation.5 | async-start | bytes 524288 | tf_op jit(solution)/shard_map/all_to_all | solution.py:158
